TPU v7x, 128 devices: a whole 4x4x4 slice. The times are simulated.
128 devices in a mesh: section: 16 (over x, z_hi, core), expert: 8 (over z_lo, y).
Axes of the slice: x: 4, y: 4, z: 4 (z_hi: 2, z_lo: 2; z = z_hi * 2 + z_lo), core: 2. Of those that a mesh axis runs over, the one named last changes fastest.
Arguments:
- grad_in: bfloat16 [16, 1024, 4096], P('section', 'expert'), may hold values from -6 to 6
- saved_inputs: bfloat16 [3, 16, 1024, 4096], P(None, 'section', 'expert'), may hold values from -6 to 6
- expert_ids: int32 [3, 16, 1024, 2], P(None, 'section', 'expert'), may hold values from 0 to 7, as said below
- slots: int32 [3, 16, 1024, 2], P(None, 'section', 'expert'), may hold values from 0 to 36, as said below
- gates: float32 [3, 16, 1024, 2], P(None, 'section', 'expert'), may hold values from 0.05 to 0.8
- w_gate: bfloat16 [16, 8, 4096, 768], P('section', 'expert'), may hold values from -0.09375 to 0.09375
- w_up: bfloat16 [16, 8, 4096, 768], P('section', 'expert'), may hold values from -0.09375 to 0.09375
- w_down: bfloat16 [16, 8, 768, 4096], P('section', 'expert'), may hold values from -0.21875 to 0.21875
Outputs:
- grad_out: bfloat16 [16, 1024, 4096], P('section', 'expert')
Inputs may be any that keep to these rules, and one draw needn't show every extreme that they name: `expert_ids`: each token names 2 different experts; every expert is named. `slots`: among the routes of the tokens of one device (aligned blocks of 128 tokens) to one expert, taken in some order, the n-th has slot min(n, 36) for n = 0, 1, ...; in every round and section some such group has more than 36 routes.
All inputs are finite; a program needn't handle non-finite values.
Results may differ from a plain program's by a relative error of at most 0.0075.
Values may be sent and summed in bfloat16 or wider, within the bound.
No kernel may reach another device: no remote copies, remote signals or barrier semaphores. Data moves between devices by JAX's collectives and lax.ppermute only.
A program may use at most 128 MiB of HBM per device.

v0:
```python
import jax
import jax.numpy as jnp
from jax import lax
from jax.sharding import PartitionSpec as P


def shifted(x, axis, by):
    devices = lax.axis_size(axis)
    return lax.ppermute(x, axis, [(i, (i + by) % devices) for i in range(devices)])


def forward_part(input_part, gate_proj, up_proj):
    pre_gate = jnp.einsum("scjl,jlh->sch", input_part, gate_proj, preferred_element_type=jnp.float32)
    pre_up = jnp.einsum("scjl,jlh->sch", input_part, up_proj, preferred_element_type=jnp.float32)
    return pre_gate, pre_up


def backward_part(grad_part, pre_gate, pre_up, gate_proj, up_proj, down_proj):
    grad_hidden = jnp.einsum("scjl,hjl->sch", grad_part, down_proj, preferred_element_type=jnp.float32)
    sigma = jax.nn.sigmoid(pre_gate)
    derivative = sigma * (1.0 + pre_gate * (1.0 - sigma))
    grad_gate = (grad_hidden * pre_up * derivative).astype(jnp.bfloat16)
    grad_up = (grad_hidden * pre_gate * sigma).astype(jnp.bfloat16)
    summed = jnp.einsum("sch,jlh->scjl", grad_gate, gate_proj, preferred_element_type=jnp.float32)
    summed = summed + jnp.einsum("sch,jlh->scjl", grad_up, up_proj, preferred_element_type=jnp.float32)
    return summed.astype(jnp.bfloat16)


def per_device(grad_in, saved_inputs, expert_ids, slots, gates, w_gate, w_up, w_down):
    groups = lax.axis_size("expert")
    rows_dev = grad_in.shape[1]
    width = grad_in.shape[2]
    rounds = saved_inputs.shape[0]
    capacity = 9 * rows_dev * expert_ids.shape[-1] // (8 * groups)
    lanes = 128
    pieces = width // lanes
    columns = groups * capacity
    hidden = w_gate.shape[-1]
    gate_proj = w_gate[0, 0].reshape(pieces, lanes, hidden)
    up_proj = w_up[0, 0].reshape(pieces, lanes, hidden)
    down_proj = w_down[0, 0].reshape(hidden, pieces, lanes)
    column_ids = jnp.arange(columns, dtype=jnp.int32)

    def route_plan(step):
        route_ids = expert_ids[step, 0]
        slot_ids = slots[step, 0]
        target = jnp.where(slot_ids < capacity, route_ids * capacity + slot_ids, -1)
        hit = target[:, :, None] == column_ids[None, None, :]
        dispatch = jnp.any(hit, axis=1).T.astype(jnp.bfloat16).reshape(groups, capacity, rows_dev)
        weights = jnp.sum(jnp.where(hit, gates[step, 0][:, :, None], 0.0), axis=1)
        weights_hi = weights.astype(jnp.bfloat16)
        weights_lo = (weights - weights_hi.astype(jnp.float32)).astype(jnp.bfloat16)
        shape = (rows_dev, groups, capacity)
        return dispatch, weights_hi.reshape(shape), weights_lo.reshape(shape)

    def collect(dispatch, rows):
        picked = jnp.einsum("ect,tjl->ecjl", dispatch, rows, preferred_element_type=jnp.float32)
        return picked.astype(jnp.bfloat16)

    def exchange(buffer):
        count = buffer.shape[1]
        flat = buffer.reshape(groups, count * pieces, lanes)
        moved = lax.all_to_all(flat, "expert", split_axis=0, concat_axis=0, tiled=True)
        return moved.reshape(groups, count, pieces, lanes)

    plans = [route_plan(step) for step in range(rounds)]
    input_buffers = [
        collect(plans[step][0], saved_inputs[step, 0].reshape(rows_dev, pieces, lanes))
        for step in range(rounds)
    ]
    first_part = exchange(input_buffers[0])
    first_part, first_block = lax.optimization_barrier((first_part, grad_in[0]))
    pre_gate, pre_up = forward_part(first_part, gate_proj, up_proj)
    bounds = [(0, capacity // 2), (capacity // 2, capacity)]

    present_block = first_block.reshape(rows_dev, pieces, lanes)
    for step in range(rounds):
        dispatch, weights_hi, weights_lo = plans[step]
        if step > 0:
            next_part, present_block = lax.optimization_barrier((next_part, present_block))
        grad_parts = [exchange(collect(dispatch[:, lo:hi], present_block)) for lo, hi in bounds]
        if step > 0:
            pre_gate, pre_up = forward_part(next_part, gate_proj, up_proj)
        results = [
            backward_part(grad_parts[i], pre_gate[:, lo:hi], pre_up[:, lo:hi], gate_proj, up_proj, down_proj)
            for i, (lo, hi) in enumerate(bounds)
        ]
        summed = present_block.astype(jnp.float32)
        for i, (lo, hi) in enumerate(bounds):
            arrived = exchange(results[i])
            if i + 1 == len(bounds) and step + 1 < rounds:
                arrived, next_buffer = lax.optimization_barrier((arrived, input_buffers[step + 1]))
                next_part = exchange(next_buffer)
            summed = summed + jnp.einsum(
                "tec,ecjl->tjl", weights_hi[:, :, lo:hi], arrived, preferred_element_type=jnp.float32
            )
            summed = summed + jnp.einsum(
                "tec,ecjl->tjl", weights_lo[:, :, lo:hi], arrived, preferred_element_type=jnp.float32
            )
        present_block = shifted(summed.astype(jnp.bfloat16), "section", -1)
    return present_block.reshape(1, rows_dev, width)


def solution(mesh):
    placed = (
        P("section", "expert", None),
        P(None, "section", "expert", None),
        P(None, "section", "expert", None),
        P(None, "section", "expert", None),
        P(None, "section", "expert", None),
        P("section", "expert", None, None),
        P("section", "expert", None, None),
        P("section", "expert", None, None),
    )
    return jax.shard_map(
        per_device,
        mesh=mesh,
        in_specs=placed,
        out_specs=P("section", "expert", None),
        check_vma=False,
    )
```

profile of v0, /device:TPU:7, one launch (start us, length us, event | category | flops | bytes accessed | tf_op | source)
XLA Modules:
  0.0 424.9 jit_solution(8575917393079977058)
XLA Ops:
  7.8 5.5 %all-to-all-start = ((bf16[8,1152,128]{2,1,0:T(8,128)(2,1)}), bf16[8,1152,128]{2,1,0:T(8,128)(2,1)S(1)}, u32[]{:S(2)}, u32[]{:S(2)}) async-start(bf16[8,1152,128]{2,1,0:T(8,128)(2,1)} %bitcast.11), calls=%async_computation | async-start | bytes 4718592 | tf_op jit(solution)/shard_map/all_to_all | solution.py:63
  13.4 7.5 %copy.199 = bf16[96,8,32,128]{3,2,1,0:T(8,128)(2,1)} copy(bf16[96,8,32,128]{3,1,2,0:T(8,128)(2,1)} %bitcast.408) | data formatting | bytes 12582912
  23.1 20.1 %all-to-all-done = bf16[8,1152,128]{2,1,0:T(8,128)(2,1)S(1)} async-done(((bf16[8,1152,128]{2,1,0:T(8,128)(2,1)}), bf16[8,1152,128]{2,1,0:T(8,128)(2,1)S(1)}, u32[]{:S(2)}, u32[]{:S(2)}) %all-to-all-start) | async-done | bytes 2359328 | tf_op jit(solution)/shard_map/all_to_all | solution.py:63
  47.1 6.1 %all-to-all-start.1 = ((bf16[8,576,128]{2,1,0:T(8,128)(2,1)}), bf16[8,576,128]{2,1,0:T(8,128)(2,1)}, u32[]{:S(2)}, u32[]{:S(2)}) async-start(bf16[8,576,128]{2,1,0:T(8,128)(2,1)} %bitcast.418), calls=%async_computation.1 | async-start | bytes 2359296 | tf_op jit(solution)/shard_map/all_to_all | solution.py:63
  55.3 7.9 %fusion.60 = f32[8,36,768]{2,1,0:T(8,128)} fusion(bf16[32,128,768,1]{2,1,0,3:T(8,128)(2,1)} %bitcast.370, bf16[8,36,32,128]{3,2,1,0:T(8,128)(2,1)S(1)} %bitcast.425), kind=kOutput, calls=%fused_computation.87 | convolution fusion | flops 1811939328 | bytes 9535488 | tf_op jit(solution)/shard_map/scjl,jlh->sch/dot_general | solution.py:14
  65.9 4.6 %all-to-all-done.1 = bf16[8,576,128]{2,1,0:T(8,128)(2,1)} async-done(((bf16[8,576,128]{2,1,0:T(8,128)(2,1)}), bf16[8,576,128]{2,1,0:T(8,128)(2,1)}, u32[]{:S(2)}, u32[]{:S(2)}) %all-to-all-start.1) | async-done | bytes 1179680 | tf_op jit(solution)/shard_map/all_to_all | solution.py:63
  74.4 6.8 %fusion.78 = f32[8,18,768]{2,1,0:T(8,128)S(1)} fusion(bf16[768,32,128]{2,1,0:T(8,128)(2,1)} %bitcast.409, bf16[8,18,32,128]{3,2,1,0:T(8,128)(2,1)} %bitcast.17), kind=kOutput, calls=%fused_computation.93 | convolution fusion | flops 905969664 | bytes 7913472 | tf_op jit(solution)/shard_map/scjl,hjl->sch/dot_general | solution.py:19
  81.2 4.6 %fusion.140 = f32[8,18,32,128]{3,1,2,0:T(8,128)S(1)} fusion(bf16[32,128,768,1]{2,1,0,3:T(8,128)(2,1)} %bitcast.436, f32[8,18,768]{2,1,0:T(8,128)S(1)} %fusion.78, f32[8,36,768]{2,1,0:T(8,128)S(1)} %copy-done.27, f32[8,36,768]{2,1,0:T(8,128)S(1)} %fusion.63), kind=kOutput, calls=%fused_computation.149 | convolution fusion | flops 907075584 | bytes 10420224 | tf_op jit(solution)/shard_map/sch,jlh->scjl/dot_general | solution.py:24
  96.1 6.8 %fusion.83 = f32[8,18,768]{2,1,0:T(8,128)S(1)} fusion(bf16[768,32,128]{2,1,0:T(8,128)(2,1)} %bitcast.410, bf16[8,18,32,128]{3,2,1,0:T(8,128)(2,1)} %bitcast.428), kind=kOutput, calls=%fused_computation.94 | convolution fusion | flops 905969664 | bytes 7913472 | tf_op jit(solution)/shard_map/scjl,hjl->sch/dot_general | solution.py:19
  103.0 4.5 %fusion.137 = f32[8,18,32,128]{3,1,2,0:T(8,128)S(1)} fusion(bf16[32,128,768,1]{2,1,0,3:T(8,128)(2,1)} %bitcast.437, f32[8,18,768]{2,1,0:T(8,128)S(1)} %fusion.83, f32[8,36,768]{2,1,0:T(8,128)S(1)} %copy-done.28, f32[8,36,768]{2,1,0:T(8,128)S(1)} %fusion.63), kind=kOutput, calls=%fused_computation.146 | convolution fusion | flops 907075584 | bytes 10420224 | tf_op jit(solution)/shard_map/sch,jlh->scjl/dot_general | solution.py:24
  113.3 4.1 all-to-all-start.5
  134.6 4.5 %all-to-all-start.3 = ((bf16[8,1152,128]{2,1,0:T(8,128)(2,1)}), bf16[8,1152,128]{2,1,0:T(8,128)(2,1)}, u32[]{:S(2)}, u32[]{:S(2)}) async-start(bf16[8,1152,128]{2,1,0:T(8,128)(2,1)} %bitcast.406), calls=%async_computation.3 | async-start | bytes 4718592 | tf_op jit(solution)/shard_map/all_to_all | solution.py:63
  144.0 36.1 %collective-permute-done = bf16[128,32,128]{2,0,1:T(8,128)(2,1)S(1)} collective-permute-done((bf16[128,32,128]{2,0,1:T(8,128)(2,1)S(1)}, bf16[128,32,128]{2,0,1:T(8,128)(2,1)S(1)}, u32[]{:S(2)}, u32[]{:S(2)}) %collective-permute-start) | collective-permute-done | bytes 1048608 | tf_op jit(solution)/shard_map/ppermute | solution.py:9
  182.5 4.5 %all-to-all-start.6 = ((bf16[8,576,128]{2,1,0:T(8,128)(2,1)}), bf16[8,576,128]{2,1,0:T(8,128)(2,1)}, u32[]{:S(2)}, u32[]{:S(2)}) async-start(bf16[8,576,128]{2,1,0:T(8,128)(2,1)} %bitcast.419), calls=%async_computation.6 | async-start | bytes 2359296 | tf_op jit(solution)/shard_map/all_to_all | solution.py:63
  187.0 7.2 %fusion.66 = f32[8,36,768]{2,1,0:T(8,128)} fusion(bf16[32,128,768,1]{2,1,0,3:T(8,128)(2,1)} %bitcast.371, bf16[8,36,32,128]{3,2,1,0:T(8,128)(2,1)} %bitcast.40), kind=kOutput, calls=%fused_computation.89 | convolution fusion | flops 1811939328 | bytes 9535488 | tf_op jit(solution)/shard_map/scjl,jlh->sch/dot_general | solution.py:14
  195.4 5.9 %fusion.69 = f32[8,36,768]{2,1,0:T(8,128)S(1)} fusion(bf16[32,128,768,1]{2,1,0,3:T(8,128)(2,1)} %bitcast.438, bf16[8,36,32,128]{3,2,1,0:T(8,128)(2,1)} %bitcast.40), kind=kOutput, calls=%fused_computation.90 | convolution fusion | flops 1811939328 | bytes 9535488 | tf_op jit(solution)/shard_map/scjl,jlh->sch/dot_general | solution.py:13
  208.3 6.8 %fusion.88 = f32[8,18,768]{2,1,0:T(8,128)S(1)} fusion(bf16[768,32,128]{2,1,0:T(8,128)(2,1)} %bitcast.411, bf16[8,18,32,128]{3,2,1,0:T(8,128)(2,1)} %bitcast.71), kind=kOutput, calls=%fused_computation.95 | convolution fusion | flops 905969664 | bytes 7913472 | tf_op jit(solution)/shard_map/scjl,hjl->sch/dot_general | solution.py:19
  215.2 4.6 %fusion.134 = f32[8,18,32,128]{3,1,2,0:T(8,128)S(1)} fusion(bf16[32,128,768,1]{2,1,0,3:T(8,128)(2,1)} %bitcast.439, f32[8,18,768]{2,1,0:T(8,128)S(1)} %fusion.88, f32[8,36,768]{2,1,0:T(8,128)S(1)} %copy-done.25, f32[8,36,768]{2,1,0:T(8,128)S(1)} %fusion.69), kind=kOutput, calls=%fused_computation.143 | convolution fusion | flops 907075584 | bytes 10420224 | tf_op jit(solution)/shard_map/sch,jlh->scjl/dot_general | solution.py:24
  230.1 6.8 %fusion.93 = f32[8,18,768]{2,1,0:T(8,128)S(1)} fusion(bf16[768,32,128]{2,1,0:T(8,128)(2,1)} %bitcast.412, bf16[8,18,32,128]{3,2,1,0:T(8,128)(2,1)} %bitcast.429), kind=kOutput, calls=%fused_computation.96 | convolution fusion | flops 905969664 | bytes 7913472 | tf_op jit(solution)/shard_map/scjl,hjl->sch/dot_general | solution.py:19
  237.0 4.5 %fusion.131 = f32[8,18,32,128]{3,1,2,0:T(8,128)S(1)} fusion(bf16[32,128,768,1]{2,1,0,3:T(8,128)(2,1)} %bitcast.440, f32[8,18,768]{2,1,0:T(8,128)S(1)} %fusion.93, f32[8,36,768]{2,1,0:T(8,128)S(1)} %copy-done.26, f32[8,36,768]{2,1,0:T(8,128)S(1)} %fusion.69), kind=kOutput, calls=%fused_computation.140 | convolution fusion | flops 907075584 | bytes 10420224 | tf_op jit(solution)/shard_map/sch,jlh->scjl/dot_general | solution.py:24
  268.4 4.4 %all-to-all-start.8 = ((bf16[8,1152,128]{2,1,0:T(8,128)(2,1)}), bf16[8,1152,128]{2,1,0:T(8,128)(2,1)}, u32[]{:S(2)}, u32[]{:S(2)}) async-start(bf16[8,1152,128]{2,1,0:T(8,128)(2,1)} %bitcast.407), calls=%async_computation.8 | async-start | bytes 4718592 | tf_op jit(solution)/shard_map/all_to_all | solution.py:63
  277.7 32.3 %collective-permute-done.1 = bf16[128,32,128]{2,0,1:T(8,128)(2,1)S(1)} collective-permute-done((bf16[128,32,128]{2,0,1:T(8,128)(2,1)S(1)}, bf16[128,32,128]{2,0,1:T(8,128)(2,1)S(1)}, u32[]{:S(2)}, u32[]{:S(2)}) %collective-permute-start.1) | collective-permute-done | bytes 1048608 | tf_op jit(solution)/shard_map/ppermute | solution.py:9
  313.3 8.4 %all-to-all-start.13 = ((bf16[8,576,128]{2,1,0:T(8,128)(2,1)}), bf16[8,576,128]{2,1,0:T(8,128)(2,1)}, u32[]{:S(2)}, u32[]{:S(2)}) async-start(bf16[8,576,128]{2,1,0:T(8,128)(2,1)} %bitcast.420), calls=%async_computation.13 | async-start | bytes 2359296 | tf_op jit(solution)/shard_map/all_to_all | solution.py:63
  321.8 7.1 %fusion.72 = f32[8,36,768]{2,1,0:T(8,128)} fusion(bf16[32,128,768,1]{2,1,0,3:T(8,128)(2,1)} %bitcast.372, bf16[8,36,32,128]{3,2,1,0:T(8,128)(2,1)} %bitcast.91), kind=kOutput, calls=%fused_computation.91 | convolution fusion | flops 1811939328 | bytes 9535488 | tf_op jit(solution)/shard_map/scjl,jlh->sch/dot_general | solution.py:14
  330.1 5.9 %fusion.75 = f32[8,36,768]{2,1,0:T(8,128)S(1)} fusion(bf16[32,128,768,1]{2,1,0,3:T(8,128)(2,1)} %bitcast.441, bf16[8,36,32,128]{3,2,1,0:T(8,128)(2,1)} %bitcast.91), kind=kOutput, calls=%fused_computation.92 | convolution fusion | flops 1811939328 | bytes 9535488 | tf_op jit(solution)/shard_map/scjl,jlh->sch/dot_general | solution.py:13
  339.1 4.0 all-to-all-start.11
  343.1 6.8 %fusion.103 = f32[8,18,768]{2,1,0:T(8,128)S(1)} fusion(bf16[768,32,128]{2,1,0:T(8,128)(2,1)} %bitcast.413, bf16[8,18,32,128]{3,2,1,0:T(8,128)(2,1)} %bitcast.147), kind=kOutput, calls=%fused_computation.98 | convolution fusion | flops 905969664 | bytes 7913472 | tf_op jit(solution)/shard_map/scjl,hjl->sch/dot_general | solution.py:19
  349.9 4.6 %fusion.125 = f32[8,18,32,128]{3,1,2,0:T(8,128)S(1)} fusion(bf16[32,128,768,1]{2,1,0,3:T(8,128)(2,1)} %bitcast.442, f32[8,18,768]{2,1,0:T(8,128)S(1)} %fusion.103, f32[8,36,768]{2,1,0:T(8,128)S(1)} %copy-done.23, f32[8,36,768]{2,1,0:T(8,128)S(1)} %fusion.75), kind=kOutput, calls=%fused_computation.134 | convolution fusion | flops 907075584 | bytes 10420224 | tf_op jit(solution)/shard_map/sch,jlh->scjl/dot_general | solution.py:24
  364.9 6.8 %fusion.98 = f32[8,18,768]{2,1,0:T(8,128)S(1)} fusion(bf16[768,32,128]{2,1,0:T(8,128)(2,1)} %bitcast.414, bf16[8,18,32,128]{3,2,1,0:T(8,128)(2,1)} %bitcast.427), kind=kOutput, calls=%fused_computation.97 | convolution fusion | flops 905969664 | bytes 7913472 | tf_op jit(solution)/shard_map/scjl,hjl->sch/dot_general | solution.py:19
  371.8 4.5 %fusion.128 = f32[8,18,32,128]{3,1,2,0:T(8,128)S(1)} fusion(bf16[32,128,768,1]{2,1,0,3:T(8,128)(2,1)} %bitcast.443, f32[8,18,768]{2,1,0:T(8,128)S(1)} %fusion.98, f32[8,36,768]{2,1,0:T(8,128)S(1)} %copy-done.24, f32[8,36,768]{2,1,0:T(8,128)S(1)} %fusion.75), kind=kOutput, calls=%fused_computation.137 | convolution fusion | flops 907075584 | bytes 10420224 | tf_op jit(solution)/shard_map/sch,jlh->scjl/dot_general | solution.py:24
  390.0 13.0 %all-to-all-done.12 = bf16[8,576,128]{2,1,0:T(8,128)(2,1)S(1)} async-done(((bf16[8,576,128]{2,1,0:T(8,128)(2,1)}), bf16[8,576,128]{2,1,0:T(8,128)(2,1)S(1)}, u32[]{:S(2)}, u32[]{:S(2)}) %all-to-all-start.12) | async-done | bytes 1179680 | tf_op jit(solution)/shard_map/all_to_all | solution.py:63
  407.9 14.9 %collective-permute-done.2 = bf16[128,32,128]{2,0,1:T(8,128)(2,1)S(1)} collective-permute-done((bf16[128,32,128]{2,0,1:T(8,128)(2,1)S(1)}, bf16[128,32,128]{2,0,1:T(8,128)(2,1)S(1)}, u32[]{:S(2)}, u32[]{:S(2)}) %collective-permute-start.2) | collective-permute-done | bytes 1048608 | tf_op jit(solution)/shard_map/ppermute | solution.py:9
  (184 shorter events, 152.0 us)
Async XLA Ops:
  4.3 113.1 %copy-start.19 = (s32[128,2]{0,1:T(2,128)}, s32[128,2]{0,1:T(2,128)S(1)}, u32[]{:S(2)}) copy-start(s32[128,2]{0,1:T(2,128)S(1)} %get-tuple-element.35) | copy-start | bytes 3076
  7.8 35.4 %all-to-all-start = ((bf16[8,1152,128]{2,1,0:T(8,128)(2,1)}), bf16[8,1152,128]{2,1,0:T(8,128)(2,1)S(1)}, u32[]{:S(2)}, u32[]{:S(2)}) async-start(bf16[8,1152,128]{2,1,0:T(8,128)(2,1)} %bitcast.11), calls=%async_computation | async-start | bytes 4718592 | tf_op jit(solution)/shard_map/all_to_all | solution.py:63
  47.1 23.4 %all-to-all-start.1 = ((bf16[8,576,128]{2,1,0:T(8,128)(2,1)}), bf16[8,576,128]{2,1,0:T(8,128)(2,1)}, u32[]{:S(2)}, u32[]{:S(2)}) async-start(bf16[8,576,128]{2,1,0:T(8,128)(2,1)} %bitcast.418), calls=%async_computation.1 | async-start | bytes 2359296 | tf_op jit(solution)/shard_map/all_to_all | solution.py:63
  53.2 10.0 %slice-start.12 = ((s8[6291456]{0:T(1024)(128)(4,1)}), s8[4194304]{0:T(1024)(128)(4,1)S(1)}, s32[]{:S(2)}) async-start(s8[6291456]{0:T(1024)(128)(4,1)} %bitcast.444), calls=%async_computation.27 | async-start | bytes 8388608
  55.3 7.9 %slice-start.13 = ((s8[6291456]{0:T(1024)(128)(4,1)}), s8[2097152]{0:T(1024)(128)(4,1)S(1)}, s32[]{:S(2)}) async-start(s8[6291456]{0:T(1024)(128)(4,1)} %bitcast.444), calls=%async_computation.28 | async-start | bytes 4194304
  70.5 21.1 %all-to-all-start.4 = ((bf16[8,576,128]{2,1,0:T(8,128)(2,1)}), bf16[8,576,128]{2,1,0:T(8,128)(2,1)S(1)}, u32[]{:S(2)}, u32[]{:S(2)}) async-start(bf16[8,576,128]{2,1,0:T(8,128)(2,1)} %bitcast.46), calls=%async_computation.4 | async-start | bytes 2359296 | tf_op jit(solution)/shard_map/all_to_all | solution.py:63
  74.3 6.9 %copy-start.27 = (f32[8,36,768]{2,1,0:T(8,128)S(1)}, f32[8,36,768]{2,1,0:T(8,128)}, u32[]{:S(2)}) copy-start(f32[8,36,768]{2,1,0:T(8,128)} %fusion.60) | copy-start | bytes 2654212
  74.4 11.5 %slice-start = ((s8[6291456]{0:T(1024)(128)(4,1)}), s8[4194304]{0:T(1024)(128)(4,1)S(1)}, s32[]{:S(2)}) async-start(s8[6291456]{0:T(1024)(128)(4,1)} %bitcast.373), calls=%async_computation.15 | async-start | bytes 8388608
  92.5 20.7 %all-to-all-start.2 = ((bf16[8,576,128]{2,1,0:T(8,128)(2,1)}), bf16[8,576,128]{2,1,0:T(8,128)(2,1)S(1)}, u32[]{:S(2)}, u32[]{:S(2)}) async-start(bf16[8,576,128]{2,1,0:T(8,128)(2,1)} %bitcast.34), calls=%async_computation.2 | async-start | bytes 2359296 | tf_op jit(solution)/shard_map/all_to_all | solution.py:63
  96.1 6.9 %copy-start.28 = (f32[8,36,768]{2,1,0:T(8,128)S(1)}, f32[8,36,768]{2,1,0:T(8,128)}, u32[]{:S(2)}) copy-start(f32[8,36,768]{2,1,0:T(8,128)} %fusion.60) | copy-start | bytes 2654212
  96.1 11.4 %slice-start.2 = ((s8[6291456]{0:T(1024)(128)(4,1)}), s8[4194304]{0:T(1024)(128)(4,1)S(1)}, s32[]{:S(2)}) async-start(s8[6291456]{0:T(1024)(128)(4,1)} %bitcast.376), calls=%async_computation.17 | async-start | bytes 8388608
  113.3 21.3 %all-to-all-start.5 = ((bf16[8,576,128]{2,1,0:T(8,128)(2,1)}), bf16[8,576,128]{2,1,0:T(8,128)(2,1)S(1)}, u32[]{:S(2)}, u32[]{:S(2)}) async-start(bf16[8,576,128]{2,1,0:T(8,128)(2,1)} %bitcast.416), calls=%async_computation.5 | async-start | bytes 2359296 | tf_op jit(solution)/shard_map/all_to_all | solution.py:63
  134.6 45.5 %all-to-all-start.3 = ((bf16[8,1152,128]{2,1,0:T(8,128)(2,1)}), bf16[8,1152,128]{2,1,0:T(8,128)(2,1)}, u32[]{:S(2)}, u32[]{:S(2)}) async-start(bf16[8,1152,128]{2,1,0:T(8,128)(2,1)} %bitcast.406), calls=%async_computation.3 | async-start | bytes 4718592 | tf_op jit(solution)/shard_map/all_to_all | solution.py:63
  142.5 37.5 %collective-permute-start = (bf16[128,32,128]{2,0,1:T(8,128)(2,1)S(1)}, bf16[128,32,128]{2,0,1:T(8,128)(2,1)S(1)}, u32[]{:S(2)}, u32[]{:S(2)}) collective-permute-start(bf16[128,32,128]{2,0,1:T(8,128)(2,1)S(1)} %fusion.32), channel_id=1, source_target_pairs={{0,120},{8,0},{16,8},{24,16},{32,24},{40,32},{48,40},{56,48},{64,5... | collective-permute-start | bytes 3145736 | tf_op jit(solution)/shard_map/ppermute | solution.py:9
  182.5 22.0 %all-to-all-start.6 = ((bf16[8,576,128]{2,1,0:T(8,128)(2,1)}), bf16[8,576,128]{2,1,0:T(8,128)(2,1)}, u32[]{:S(2)}, u32[]{:S(2)}) async-start(bf16[8,576,128]{2,1,0:T(8,128)(2,1)} %bitcast.419), calls=%async_computation.6 | async-start | bytes 2359296 | tf_op jit(solution)/shard_map/all_to_all | solution.py:63
  204.5 21.0 %all-to-all-start.9 = ((bf16[8,576,128]{2,1,0:T(8,128)(2,1)}), bf16[8,576,128]{2,1,0:T(8,128)(2,1)S(1)}, u32[]{:S(2)}, u32[]{:S(2)}) async-start(bf16[8,576,128]{2,1,0:T(8,128)(2,1)} %bitcast.96), calls=%async_computation.9 | async-start | bytes 2359296 | tf_op jit(solution)/shard_map/all_to_all | solution.py:63
  208.3 6.9 %copy-start.25 = (f32[8,36,768]{2,1,0:T(8,128)S(1)}, f32[8,36,768]{2,1,0:T(8,128)}, u32[]{:S(2)}) copy-start(f32[8,36,768]{2,1,0:T(8,128)} %fusion.66) | copy-start | bytes 2654212
  208.3 11.5 %slice-start.4 = ((s8[6291456]{0:T(1024)(128)(4,1)}), s8[4194304]{0:T(1024)(128)(4,1)S(1)}, s32[]{:S(2)}) async-start(s8[6291456]{0:T(1024)(128)(4,1)} %bitcast.379), calls=%async_computation.19 | async-start | bytes 8388608
  226.5 20.8 %all-to-all-start.7 = ((bf16[8,576,128]{2,1,0:T(8,128)(2,1)}), bf16[8,576,128]{2,1,0:T(8,128)(2,1)S(1)}, u32[]{:S(2)}, u32[]{:S(2)}) async-start(bf16[8,576,128]{2,1,0:T(8,128)(2,1)} %bitcast.83), calls=%async_computation.7 | async-start | bytes 2359296 | tf_op jit(solution)/shard_map/all_to_all | solution.py:63
  230.1 11.4 %slice-start.6 = ((s8[6291456]{0:T(1024)(128)(4,1)}), s8[4194304]{0:T(1024)(128)(4,1)S(1)}, s32[]{:S(2)}) async-start(s8[6291456]{0:T(1024)(128)(4,1)} %bitcast.382), calls=%async_computation.21 | async-start | bytes 8388608
  247.3 21.1 %all-to-all-start.10 = ((bf16[8,576,128]{2,1,0:T(8,128)(2,1)}), bf16[8,576,128]{2,1,0:T(8,128)(2,1)S(1)}, u32[]{:S(2)}, u32[]{:S(2)}) async-start(bf16[8,576,128]{2,1,0:T(8,128)(2,1)} %bitcast.415), calls=%async_computation.10 | async-start | bytes 2359296 | tf_op jit(solution)/shard_map/all_to_all | solution.py:63
  268.4 42.5 %all-to-all-start.8 = ((bf16[8,1152,128]{2,1,0:T(8,128)(2,1)}), bf16[8,1152,128]{2,1,0:T(8,128)(2,1)}, u32[]{:S(2)}, u32[]{:S(2)}) async-start(bf16[8,1152,128]{2,1,0:T(8,128)(2,1)} %bitcast.407), calls=%async_computation.8 | async-start | bytes 4718592 | tf_op jit(solution)/shard_map/all_to_all | solution.py:63
  276.8 33.2 %collective-permute-start.1 = (bf16[128,32,128]{2,0,1:T(8,128)(2,1)S(1)}, bf16[128,32,128]{2,0,1:T(8,128)(2,1)S(1)}, u32[]{:S(2)}, u32[]{:S(2)}) collective-permute-start(bf16[128,32,128]{2,0,1:T(8,128)(2,1)S(1)} %fusion.31), channel_id=1, source_target_pairs={{0,120},{8,0},{16,8},{24,16},{32,24},{40,32},{48,40},{56,48},{64,5... | collective-permute-start | bytes 3145736 | tf_op jit(solution)/shard_map/ppermute | solution.py:9
  313.3 25.7 %all-to-all-start.13 = ((bf16[8,576,128]{2,1,0:T(8,128)(2,1)}), bf16[8,576,128]{2,1,0:T(8,128)(2,1)}, u32[]{:S(2)}, u32[]{:S(2)}) async-start(bf16[8,576,128]{2,1,0:T(8,128)(2,1)} %bitcast.420), calls=%async_computation.13 | async-start | bytes 2359296 | tf_op jit(solution)/shard_map/all_to_all | solution.py:63
  339.1 21.2 %all-to-all-start.11 = ((bf16[8,576,128]{2,1,0:T(8,128)(2,1)}), bf16[8,576,128]{2,1,0:T(8,128)(2,1)S(1)}, u32[]{:S(2)}, u32[]{:S(2)}) async-start(bf16[8,576,128]{2,1,0:T(8,128)(2,1)} %bitcast.123), calls=%async_computation.11 | async-start | bytes 2359296 | tf_op jit(solution)/shard_map/all_to_all | solution.py:63
  343.0 6.9 %copy-start.23 = (f32[8,36,768]{2,1,0:T(8,128)S(1)}, f32[8,36,768]{2,1,0:T(8,128)}, u32[]{:S(2)}) copy-start(f32[8,36,768]{2,1,0:T(8,128)} %fusion.72) | copy-start | bytes 2654212
  343.1 11.5 %slice-start.8 = ((s8[6291456]{0:T(1024)(128)(4,1)}), s8[4194304]{0:T(1024)(128)(4,1)S(1)}, s32[]{:S(2)}) async-start(s8[6291456]{0:T(1024)(128)(4,1)} %bitcast.385), calls=%async_computation.23 | async-start | bytes 8388608
  361.3 20.7 %all-to-all-start.14 = ((bf16[8,576,128]{2,1,0:T(8,128)(2,1)}), bf16[8,576,128]{2,1,0:T(8,128)(2,1)S(1)}, u32[]{:S(2)}, u32[]{:S(2)}) async-start(bf16[8,576,128]{2,1,0:T(8,128)(2,1)} %bitcast.155), calls=%async_computation.14 | async-start | bytes 2359296 | tf_op jit(solution)/shard_map/all_to_all | solution.py:63
  364.9 6.9 %copy-start.24 = (f32[8,36,768]{2,1,0:T(8,128)S(1)}, f32[8,36,768]{2,1,0:T(8,128)}, u32[]{:S(2)}) copy-start(f32[8,36,768]{2,1,0:T(8,128)} %fusion.72) | copy-start | bytes 2654212
  364.9 11.4 %slice-start.10 = ((s8[6291456]{0:T(1024)(128)(4,1)}), s8[4194304]{0:T(1024)(128)(4,1)S(1)}, s32[]{:S(2)}) async-start(s8[6291456]{0:T(1024)(128)(4,1)} %bitcast.388), calls=%async_computation.25 | async-start | bytes 8388608
  382.0 20.9 %all-to-all-start.12 = ((bf16[8,576,128]{2,1,0:T(8,128)(2,1)}), bf16[8,576,128]{2,1,0:T(8,128)(2,1)S(1)}, u32[]{:S(2)}, u32[]{:S(2)}) async-start(bf16[8,576,128]{2,1,0:T(8,128)(2,1)} %bitcast.417), calls=%async_computation.12 | async-start | bytes 2359296 | tf_op jit(solution)/shard_map/all_to_all | solution.py:63
  407.0 15.8 %collective-permute-start.2 = (bf16[128,32,128]{2,0,1:T(8,128)(2,1)S(1)}, bf16[128,32,128]{2,0,1:T(8,128)(2,1)S(1)}, u32[]{:S(2)}, u32[]{:S(2)}) collective-permute-start(bf16[128,32,128]{2,0,1:T(8,128)(2,1)S(1)} %fusion.30), channel_id=1, source_target_pairs={{0,120},{8,0},{16,8},{24,16},{32,24},{40,32},{48,40},{56,48},{64,5... | collective-permute-start | bytes 3145736 | tf_op jit(solution)/shard_map/ppermute | solution.py:9
  (29 other events, 75.2 us)
where the time goes:
time: 433 us; the launch traced here: 425 us
  waiting for transfers between devices  146 us (34%)
  matrix products  142 us (33%)
  starting transfers between devices  70.6 us (16%)
  local copies, waits for them, and re-layouts  58.7 us (14%)
  other arithmetic  7.13 us (2%)
    ppermute x3, waiting for transfers between devices, shifted(): lax.ppermute(x, axis, [(i, (i + by) % devices) for i in range(devices)])  83.2 us
    all_to_all x15, starting transfers between devices, exchange(): lax.all_to_all(flat, 'expert', split_axis=0, concat_axis=0, tiled=True)  67.4 us
    all_to_all x15, waiting for transfers between devices, exchange(): lax.all_to_all(flat, 'expert', split_axis=0, concat_axis=0, tiled=True)  62.5 us
    dot_general x6, matrix products, backward_part(): jnp.einsum('scjl,hjl->sch', grad_part, down_proj, preferred_element_type=...  41 us
    dot_general x6, matrix products, backward_part(): jnp.einsum('sch,jlh->scjl', grad_gate, gate_proj, preferred_element_type=...  27.2 us
    unnamed x91, local copies, waits for them, and re-layouts  23.8 us
    dot_general x3, matrix products, forward_part(): jnp.einsum('scjl,jlh->sch', input_part, up_proj, preferred_element_type=j...  22.1 us
    dot_general x3, matrix products, forward_part(): jnp.einsum('scjl,jlh->sch', input_part, gate_proj, preferred_element_type...  14.4 us
  transfers between devices with their start and end apart: 18, of which 17 were waited for; matrix products, arithmetic and copies ran while one was open for 42% of the time, Pallas kernels for 0%

commit v1 on v0

--- a/solution.py
+++ b/solution.py
@@ -68,17 +68,19 @@
         collect(plans[step][0], saved_inputs[step, 0].reshape(rows_dev, pieces, lanes))
         for step in range(rounds)
     ]
-    first_part = exchange(input_buffers[0])
-    first_part, first_block = lax.optimization_barrier((first_part, grad_in[0]))
-    pre_gate, pre_up = forward_part(first_part, gate_proj, up_proj)
     bounds = [(0, capacity // 2), (capacity // 2, capacity)]
+    present_block = grad_in[0].reshape(rows_dev, pieces, lanes)
+    first = exchange(
+        jnp.concatenate([input_buffers[0], collect(plans[0][0][:, : bounds[0][1]], present_block)], axis=1)
+    )
+    pre_gate, pre_up = forward_part(first[:, :capacity], gate_proj, up_proj)
 
-    present_block = first_block.reshape(rows_dev, pieces, lanes)
     for step in range(rounds):
         dispatch, weights_hi, weights_lo = plans[step]
-        if step > 0:
-            next_part, present_block = lax.optimization_barrier((next_part, present_block))
-        grad_parts = [exchange(collect(dispatch[:, lo:hi], present_block)) for lo, hi in bounds]
+        grad_parts = [
+            first[:, capacity:] if step == 0 and i == 0 else exchange(collect(dispatch[:, lo:hi], present_block))
+            for i, (lo, hi) in enumerate(bounds)
+        ]
         if step > 0:
             pre_gate, pre_up = forward_part(next_part, gate_proj, up_proj)
         results = [
@@ -87,10 +89,12 @@
         ]
         summed = present_block.astype(jnp.float32)
         for i, (lo, hi) in enumerate(bounds):
-            arrived = exchange(results[i])
             if i + 1 == len(bounds) and step + 1 < rounds:
-                arrived, next_buffer = lax.optimization_barrier((arrived, input_buffers[step + 1]))
-                next_part = exchange(next_buffer)
+                both = exchange(jnp.concatenate([results[i], input_buffers[step + 1]], axis=1))
+                arrived = both[:, : hi - lo]
+                next_part = both[:, hi - lo :]
+            else:
+                arrived = exchange(results[i])
             summed = summed + jnp.einsum(
                 "tec,ecjl->tjl", weights_hi[:, :, lo:hi], arrived, preferred_element_type=jnp.float32
             )

time: 433 us -> 470 us (1.085)
  the two profiles are of different devices: /device:TPU:7 before, /device:TPU:1 now
where the time goes in v1:
time: 470 us; the launch traced here: 464 us
  waiting for transfers between devices  179 us (38%)
  matrix products  139 us (30%)
  starting transfers between devices  80.9 us (17%)
  local copies, waits for them, and re-layouts  58.3 us (12%)
  other arithmetic  6.03 us (1%)
    all_to_all x12, waiting for transfers between devices, exchange(): lax.all_to_all(flat, 'expert', split_axis=0, concat_axis=0, tiled=True)  143 us
    all_to_all x12, starting transfers between devices, exchange(): lax.all_to_all(flat, 'expert', split_axis=0, concat_axis=0, tiled=True)  78 us
    dot_general x6, matrix products, backward_part(): jnp.einsum('scjl,hjl->sch', grad_part, down_proj, preferred_element_type=...  38.5 us
    ppermute x3, waiting for transfers between devices, shifted(): lax.ppermute(x, axis, [(i, (i + by) % devices) for i in range(devices)])  36.2 us
    dot_general x6, matrix products, backward_part(): jnp.einsum('sch,jlh->scjl', grad_gate, gate_proj, preferred_element_type=...  25.5 us
    unnamed x95, local copies, waits for them, and re-layouts  19.8 us
    dot_general x3, matrix products, forward_part(): jnp.einsum('scjl,jlh->sch', input_part, gate_proj, preferred_element_type...  19.1 us
    dot_general x3, matrix products, forward_part(): jnp.einsum('scjl,jlh->sch', input_part, up_proj, preferred_element_type=j...  13.5 us
  transfers between devices with their start and end apart: 15, of which 14 were waited for; matrix products, arithmetic and copies ran while one was open for 32% of the time, Pallas kernels for 0%

profile of v1, /device:TPU:1, one launch (start us, length us, event | category | flops | bytes accessed | tf_op | source)
XLA Modules:
  0.0 464.5 jit_solution(12459167294452267159)
XLA Ops:
  4.3 6.4 %all-to-all-start.2 = ((bf16[8,576,128]{2,1,0:T(8,128)(2,1)}), bf16[8,576,128]{2,1,0:T(8,128)(2,1)}, u32[]{:S(2)}, u32[]{:S(2)}) async-start(bf16[8,576,128]{2,1,0:T(8,128)(2,1)} %bitcast.40), calls=%async_computation.2 | async-start | bytes 2359296 | tf_op jit(solution)/shard_map/all_to_all | solution.py:63
  21.0 7.0 %all-to-all-done.2 = bf16[8,576,128]{2,1,0:T(8,128)(2,1)} async-done(((bf16[8,576,128]{2,1,0:T(8,128)(2,1)}), bf16[8,576,128]{2,1,0:T(8,128)(2,1)}, u32[]{:S(2)}, u32[]{:S(2)}) %all-to-all-start.2) | async-done | bytes 1179680 | tf_op jit(solution)/shard_map/all_to_all | solution.py:63
  28.0 5.0 %all-to-all-start = ((bf16[8,1728,128]{2,1,0:T(8,128)(2,1)}), bf16[8,1728,128]{2,1,0:T(8,128)(2,1)}, u32[]{:S(2)}, u32[]{:S(2)}) async-start(bf16[8,1728,128]{2,1,0:T(8,128)(2,1)} %bitcast.397), calls=%async_computation | async-start | bytes 7077888 | tf_op jit(solution)/shard_map/all_to_all | solution.py:63
  33.0 7.5 %copy.193 = bf16[96,8,32,128]{3,2,1,0:T(8,128)(2,1)} copy(bf16[96,8,32,128]{3,1,2,0:T(8,128)(2,1)} %bitcast.398) | data formatting | bytes 12582912
  43.6 7.5 %fusion.83 = f32[8,18,768]{2,1,0:T(8,128)} fusion(bf16[768,32,128]{2,1,0:T(8,128)(2,1)} %bitcast.399, bf16[8,18,32,128]{3,2,1,0:T(8,128)(2,1)} %bitcast.41), kind=kOutput, calls=%fused_computation.97 | convolution fusion | flops 905969664 | bytes 7913472 | tf_op jit(solution)/shard_map/scjl,hjl->sch/dot_general | solution.py:19
  51.1 24.5 %all-to-all-done = bf16[8,1728,128]{2,1,0:T(8,128)(2,1)} async-done(((bf16[8,1728,128]{2,1,0:T(8,128)(2,1)}), bf16[8,1728,128]{2,1,0:T(8,128)(2,1)}, u32[]{:S(2)}, u32[]{:S(2)}) %all-to-all-start) | async-done | bytes 3538976 | tf_op jit(solution)/shard_map/all_to_all | solution.py:63
  79.4 5.9 %fusion.63 = f32[8,36,768]{2,1,0:T(8,128)S(1)} fusion(bf16[32,128,768,1]{2,1,0,3:T(8,128)(2,1)} %bitcast.422, bf16[8,36,32,128]{3,2,1,0:T(8,128)(2,1)S(1)} %slice.195), kind=kOutput, calls=%fused_computation.91 | convolution fusion | flops 1811939328 | bytes 9535488 | tf_op jit(solution)/shard_map/scjl,jlh->sch/dot_general | solution.py:13
  97.5 13.5 %all-to-all-start.1 = ((bf16[8,576,128]{2,1,0:T(8,128)(2,1)}), bf16[8,576,128]{2,1,0:T(8,128)(2,1)}, u32[]{:S(2)}, u32[]{:S(2)}) async-start(bf16[8,576,128]{2,1,0:T(8,128)(2,1)} %bitcast.408), calls=%async_computation.1 | async-start | bytes 2359296 | tf_op jit(solution)/shard_map/all_to_all | solution.py:63
  111.0 5.1 %fusion.137 = f32[8,18,32,128]{3,1,2,0:T(8,128)S(1)} fusion(bf16[32,128,768,1]{2,1,0,3:T(8,128)(2,1)} %bitcast.423, f32[8,18,768]{2,1,0:T(8,128)} %fusion.83, f32[8,36,768]{2,1,0:T(8,128)} %copy-done.26, f32[8,36,768]{2,1,0:T(8,128)} %copy-done.12), kind=kOutput, calls=%fused_computation.149 | convolution fusion | flops 907075584 | bytes 10420224 | tf_op jit(solution)/shard_map/sch,jlh->scjl/dot_general | solution.py:24
  122.5 5.8 %all-to-all-done.1 = bf16[8,576,128]{2,1,0:T(8,128)(2,1)} async-done(((bf16[8,576,128]{2,1,0:T(8,128)(2,1)}), bf16[8,576,128]{2,1,0:T(8,128)(2,1)}, u32[]{:S(2)}, u32[]{:S(2)}) %all-to-all-start.1) | async-done | bytes 1179680 | tf_op jit(solution)/shard_map/all_to_all | solution.py:63
  128.3 4.6 all-to-all-start.3
  142.5 33.0 %all-to-all-done.3 = bf16[8,1728,128]{2,1,0:T(8,128)(2,1)} async-done(((bf16[8,1728,128]{2,1,0:T(8,128)(2,1)}), bf16[8,1728,128]{2,1,0:T(8,128)(2,1)}, u32[]{:S(2)}, u32[]{:S(2)}) %all-to-all-start.3) | async-done | bytes 3538976 | tf_op jit(solution)/shard_map/all_to_all | solution.py:63
  183.8 5.6 %fusion.69 = f32[8,36,768]{2,1,0:T(8,128)S(1)} fusion(bf16[32,128,768,1]{2,1,0,3:T(8,128)(2,1)} %bitcast.424, bf16[8,36,32,128]{3,2,1,0:T(8,128)(2,1)S(1)} %slice.207), kind=kOutput, calls=%fused_computation.93 | convolution fusion | flops 1811939328 | bytes 9535488 | tf_op jit(solution)/shard_map/scjl,jlh->sch/dot_general | solution.py:13
  189.4 10.1 %collective-permute-done = bf16[128,32,128]{2,0,1:T(8,128)(2,1)S(1)} collective-permute-done((bf16[128,32,128]{2,0,1:T(8,128)(2,1)S(1)}, bf16[128,32,128]{2,0,1:T(8,128)(2,1)S(1)}, u32[]{:S(2)}, u32[]{:S(2)}) %collective-permute-start) | collective-permute-done | bytes 1048608 | tf_op jit(solution)/shard_map/ppermute | solution.py:9
  201.3 14.0 %all-to-all-start.4 = ((bf16[8,576,128]{2,1,0:T(8,128)(2,1)}), bf16[8,576,128]{2,1,0:T(8,128)(2,1)S(1)}, u32[]{:S(2)}, u32[]{:S(2)}) async-start(bf16[8,576,128]{2,1,0:T(8,128)(2,1)} %bitcast.67), calls=%async_computation.4 | async-start | bytes 2359296 | tf_op jit(solution)/shard_map/all_to_all | solution.py:63
  215.2 7.1 %fusion.66 = f32[8,36,768]{2,1,0:T(8,128)} fusion(bf16[32,128,768,1]{2,1,0,3:T(8,128)(2,1)} %bitcast.363, bf16[8,36,32,128]{3,2,1,0:T(8,128)(2,1)} %copy-done.8), kind=kOutput, calls=%fused_computation.92 | convolution fusion | flops 1811939328 | bytes 9535488 | tf_op jit(solution)/shard_map/scjl,jlh->sch/dot_general | solution.py:14
  224.2 8.2 %all-to-all-done.4 = bf16[8,576,128]{2,1,0:T(8,128)(2,1)S(1)} async-done(((bf16[8,576,128]{2,1,0:T(8,128)(2,1)}), bf16[8,576,128]{2,1,0:T(8,128)(2,1)S(1)}, u32[]{:S(2)}, u32[]{:S(2)}) %all-to-all-start.4) | async-done | bytes 1179680 | tf_op jit(solution)/shard_map/all_to_all | solution.py:63
  237.1 6.8 %fusion.88 = f32[8,18,768]{2,1,0:T(8,128)S(1)} fusion(bf16[768,32,128]{2,1,0:T(8,128)(2,1)} %bitcast.400, bf16[8,18,32,128]{3,2,1,0:T(8,128)(2,1)} %bitcast.415), kind=kOutput, calls=%fused_computation.98 | convolution fusion | flops 905969664 | bytes 7913472 | tf_op jit(solution)/shard_map/scjl,hjl->sch/dot_general | solution.py:19
  243.9 4.5 fusion.134
  259.1 6.8 %fusion.93 = f32[8,18,768]{2,1,0:T(8,128)S(1)} fusion(bf16[768,32,128]{2,1,0:T(8,128)(2,1)} %bitcast.401, bf16[8,18,32,128]{3,2,1,0:T(8,128)(2,1)} %bitcast.414), kind=kOutput, calls=%fused_computation.99 | convolution fusion | flops 905969664 | bytes 7913472 | tf_op jit(solution)/shard_map/scjl,hjl->sch/dot_general | solution.py:19
  265.9 4.6 fusion.131
  276.8 5.1 %all-to-all-start.7 = ((bf16[8,1728,128]{2,1,0:T(8,128)(2,1)}), bf16[8,1728,128]{2,1,0:T(8,128)(2,1)}, u32[]{:S(2)}, u32[]{:S(2)}) async-start(bf16[8,1728,128]{2,1,0:T(8,128)(2,1)} %bitcast.396), calls=%async_computation.7 | async-start | bytes 7077888 | tf_op jit(solution)/shard_map/all_to_all | solution.py:63
  286.5 38.0 %all-to-all-done.7 = bf16[8,1728,128]{2,1,0:T(8,128)(2,1)} async-done(((bf16[8,1728,128]{2,1,0:T(8,128)(2,1)}), bf16[8,1728,128]{2,1,0:T(8,128)(2,1)}, u32[]{:S(2)}, u32[]{:S(2)}) %all-to-all-start.7) | async-done | bytes 3538976 | tf_op jit(solution)/shard_map/all_to_all | solution.py:63
  336.9 11.2 %collective-permute-done.1 = bf16[128,32,128]{2,0,1:T(8,128)(2,1)S(1)} collective-permute-done((bf16[128,32,128]{2,0,1:T(8,128)(2,1)S(1)}, bf16[128,32,128]{2,0,1:T(8,128)(2,1)S(1)}, u32[]{:S(2)}, u32[]{:S(2)}) %collective-permute-start.1) | collective-permute-done | bytes 1048608 | tf_op jit(solution)/shard_map/ppermute | solution.py:9
  349.9 11.1 %all-to-all-start.8 = ((bf16[8,576,128]{2,1,0:T(8,128)(2,1)}), bf16[8,576,128]{2,1,0:T(8,128)(2,1)}, u32[]{:S(2)}, u32[]{:S(2)}) async-start(bf16[8,576,128]{2,1,0:T(8,128)(2,1)} %bitcast.116), calls=%async_computation.8 | async-start | bytes 2359296 | tf_op jit(solution)/shard_map/all_to_all | solution.py:63
  361.0 7.6 %fusion.75 = f32[8,36,768]{2,1,0:T(8,128)} fusion(bf16[32,128,768,1]{2,1,0,3:T(8,128)(2,1)} %bitcast.427, bf16[8,36,32,128]{3,2,1,0:T(8,128)(2,1)S(1)} %copy-done.10), kind=kOutput, calls=%fused_computation.95 | convolution fusion | flops 1811939328 | bytes 9535488 | tf_op jit(solution)/shard_map/scjl,jlh->sch/dot_general | solution.py:13
  370.5 7.9 %all-to-all-done.8 = bf16[8,576,128]{2,1,0:T(8,128)(2,1)} async-done(((bf16[8,576,128]{2,1,0:T(8,128)(2,1)}), bf16[8,576,128]{2,1,0:T(8,128)(2,1)}, u32[]{:S(2)}, u32[]{:S(2)}) %all-to-all-start.8) | async-done | bytes 1179680 | tf_op jit(solution)/shard_map/all_to_all | solution.py:63
  382.0 6.8 %fusion.98 = f32[8,18,768]{2,1,0:T(8,128)S(1)} fusion(bf16[768,32,128]{2,1,0:T(8,128)(2,1)} %bitcast.402, bf16[8,18,32,128]{3,2,1,0:T(8,128)(2,1)} %bitcast.117), kind=kOutput, calls=%fused_computation.100 | convolution fusion | flops 905969664 | bytes 7913472 | tf_op jit(solution)/shard_map/scjl,hjl->sch/dot_general | solution.py:19
  404.1 6.8 %fusion.103 = f32[8,18,768]{2,1,0:T(8,128)S(1)} fusion(bf16[768,32,128]{2,1,0:T(8,128)(2,1)} %bitcast.403, bf16[8,18,32,128]{3,2,1,0:T(8,128)(2,1)} %bitcast.413), kind=kOutput, calls=%fused_computation.101 | convolution fusion | flops 905969664 | bytes 7913472 | tf_op jit(solution)/shard_map/scjl,hjl->sch/dot_general | solution.py:19
  410.9 4.6 fusion.125
  430.3 11.7 %all-to-all-done.11 = bf16[8,576,128]{2,1,0:T(8,128)(2,1)S(1)} async-done(((bf16[8,576,128]{2,1,0:T(8,128)(2,1)}), bf16[8,576,128]{2,1,0:T(8,128)(2,1)S(1)}, u32[]{:S(2)}, u32[]{:S(2)}) %all-to-all-start.11) | async-done | bytes 1179680 | tf_op jit(solution)/shard_map/all_to_all | solution.py:63
  447.2 14.9 %collective-permute-done.2 = bf16[128,32,128]{2,0,1:T(8,128)(2,1)S(1)} collective-permute-done((bf16[128,32,128]{2,0,1:T(8,128)(2,1)S(1)}, bf16[128,32,128]{2,0,1:T(8,128)(2,1)S(1)}, u32[]{:S(2)}, u32[]{:S(2)}) %collective-permute-start.2) | collective-permute-done | bytes 1048608 | tf_op jit(solution)/shard_map/ppermute | solution.py:9
  (190 shorter events, 143.6 us)
Async XLA Ops:
  4.3 23.7 %all-to-all-start.2 = ((bf16[8,576,128]{2,1,0:T(8,128)(2,1)}), bf16[8,576,128]{2,1,0:T(8,128)(2,1)}, u32[]{:S(2)}, u32[]{:S(2)}) async-start(bf16[8,576,128]{2,1,0:T(8,128)(2,1)} %bitcast.40), calls=%async_computation.2 | async-start | bytes 2359296 | tf_op jit(solution)/shard_map/all_to_all | solution.py:63
  28.0 47.6 %all-to-all-start = ((bf16[8,1728,128]{2,1,0:T(8,128)(2,1)}), bf16[8,1728,128]{2,1,0:T(8,128)(2,1)}, u32[]{:S(2)}, u32[]{:S(2)}) async-start(bf16[8,1728,128]{2,1,0:T(8,128)(2,1)} %bitcast.397), calls=%async_computation | async-start | bytes 7077888 | tf_op jit(solution)/shard_map/all_to_all | solution.py:63
  77.7 7.6 %slice-start = ((s8[6291456]{0:T(1024)(128)(4,1)}), s8[4194304]{0:T(1024)(128)(4,1)S(1)}, s32[]{:S(2)}) async-start(s8[6291456]{0:T(1024)(128)(4,1)} %bitcast.364), calls=%async_computation.12 | async-start | bytes 8388608
  79.3 8.7 %slice-start.14 = ((s8[6291456]{0:T(1024)(128)(4,1)}), s8[4194304]{0:T(1024)(128)(4,1)S(1)}, s32[]{:S(2)}) async-start(s8[6291456]{0:T(1024)(128)(4,1)} %bitcast.404), calls=%async_computation.26 | async-start | bytes 8388608
  85.3 8.8 %copy-start.12 = (f32[8,36,768]{2,1,0:T(8,128)}, f32[8,36,768]{2,1,0:T(8,128)S(1)}, u32[]{:S(2)}) copy-start(f32[8,36,768]{2,1,0:T(8,128)S(1)} %fusion.63) | copy-start | bytes 2654212
  97.5 18.6 %slice-start.2 = ((s8[6291456]{0:T(1024)(128)(4,1)}), s8[2097152]{0:T(1024)(128)(4,1)S(1)}, s32[]{:S(2)}) async-start(s8[6291456]{0:T(1024)(128)(4,1)} %bitcast.368), calls=%async_computation.14 | async-start | bytes 4194304
  97.5 30.8 %all-to-all-start.1 = ((bf16[8,576,128]{2,1,0:T(8,128)(2,1)}), bf16[8,576,128]{2,1,0:T(8,128)(2,1)}, u32[]{:S(2)}, u32[]{:S(2)}) async-start(bf16[8,576,128]{2,1,0:T(8,128)(2,1)} %bitcast.408), calls=%async_computation.1 | async-start | bytes 2359296 | tf_op jit(solution)/shard_map/all_to_all | solution.py:63
  128.3 47.2 %all-to-all-start.3 = ((bf16[8,1728,128]{2,1,0:T(8,128)(2,1)}), bf16[8,1728,128]{2,1,0:T(8,128)(2,1)}, u32[]{:S(2)}, u32[]{:S(2)}) async-start(bf16[8,1728,128]{2,1,0:T(8,128)(2,1)} %bitcast.395), calls=%async_computation.3 | async-start | bytes 7077888 | tf_op jit(solution)/shard_map/all_to_all | solution.py:63
  182.9 16.6 %collective-permute-start = (bf16[128,32,128]{2,0,1:T(8,128)(2,1)S(1)}, bf16[128,32,128]{2,0,1:T(8,128)(2,1)S(1)}, u32[]{:S(2)}, u32[]{:S(2)}) collective-permute-start(bf16[128,32,128]{2,0,1:T(8,128)(2,1)S(1)} %fusion.32), channel_id=1, source_target_pairs={{0,120},{8,0},{16,8},{24,16},{32,24},{40,32},{48,40},{56,48},{64,5... | collective-permute-start | bytes 3145736 | tf_op jit(solution)/shard_map/ppermute | solution.py:9
  201.3 31.2 %all-to-all-start.4 = ((bf16[8,576,128]{2,1,0:T(8,128)(2,1)}), bf16[8,576,128]{2,1,0:T(8,128)(2,1)S(1)}, u32[]{:S(2)}, u32[]{:S(2)}) async-start(bf16[8,576,128]{2,1,0:T(8,128)(2,1)} %bitcast.67), calls=%async_computation.4 | async-start | bytes 2359296 | tf_op jit(solution)/shard_map/all_to_all | solution.py:63
  233.5 20.7 %all-to-all-start.6 = ((bf16[8,576,128]{2,1,0:T(8,128)(2,1)}), bf16[8,576,128]{2,1,0:T(8,128)(2,1)S(1)}, u32[]{:S(2)}, u32[]{:S(2)}) async-start(bf16[8,576,128]{2,1,0:T(8,128)(2,1)} %bitcast.90), calls=%async_computation.6 | async-start | bytes 2359296 | tf_op jit(solution)/shard_map/all_to_all | solution.py:63
  237.0 6.9 %copy-start.24 = (f32[8,36,768]{2,1,0:T(8,128)S(1)}, f32[8,36,768]{2,1,0:T(8,128)}, u32[]{:S(2)}) copy-start(f32[8,36,768]{2,1,0:T(8,128)} %fusion.66) | copy-start | bytes 2654212
  237.0 11.4 %slice-start.4 = ((s8[6291456]{0:T(1024)(128)(4,1)}), s8[4194304]{0:T(1024)(128)(4,1)S(1)}, s32[]{:S(2)}) async-start(s8[6291456]{0:T(1024)(128)(4,1)} %bitcast.371), calls=%async_computation.16 | async-start | bytes 8388608
  255.3 21.5 %all-to-all-start.5 = ((bf16[8,576,128]{2,1,0:T(8,128)(2,1)}), bf16[8,576,128]{2,1,0:T(8,128)(2,1)S(1)}, u32[]{:S(2)}, u32[]{:S(2)}) async-start(bf16[8,576,128]{2,1,0:T(8,128)(2,1)} %bitcast.80), calls=%async_computation.5 | async-start | bytes 2359296 | tf_op jit(solution)/shard_map/all_to_all | solution.py:63
  259.0 6.9 %copy-start.25 = (f32[8,36,768]{2,1,0:T(8,128)S(1)}, f32[8,36,768]{2,1,0:T(8,128)}, u32[]{:S(2)}) copy-start(f32[8,36,768]{2,1,0:T(8,128)} %fusion.66) | copy-start | bytes 2654212
  259.1 11.5 %slice-start.6 = ((s8[6291456]{0:T(1024)(128)(4,1)}), s8[4194304]{0:T(1024)(128)(4,1)S(1)}, s32[]{:S(2)}) async-start(s8[6291456]{0:T(1024)(128)(4,1)} %bitcast.374), calls=%async_computation.18 | async-start | bytes 8388608
  276.8 47.7 %all-to-all-start.7 = ((bf16[8,1728,128]{2,1,0:T(8,128)(2,1)}), bf16[8,1728,128]{2,1,0:T(8,128)(2,1)}, u32[]{:S(2)}, u32[]{:S(2)}) async-start(bf16[8,1728,128]{2,1,0:T(8,128)(2,1)} %bitcast.396), calls=%async_computation.7 | async-start | bytes 7077888 | tf_op jit(solution)/shard_map/all_to_all | solution.py:63
  326.0 7.2 %slice-start.8 = ((s8[6291456]{0:T(1024)(128)(4,1)}), s8[4194304]{0:T(1024)(128)(4,1)S(1)}, s32[]{:S(2)}) async-start(s8[6291456]{0:T(1024)(128)(4,1)} %bitcast.377), calls=%async_computation.20 | async-start | bytes 8388608
  332.0 16.0 %copy-start.19 = (pred[8,36,128]{2,1,0:T(8,128)(4,1)S(1)}, pred[8,36,128]{2,1,0:T(8,128)(4,1)}, u32[]{:S(2)}) copy-start(pred[8,36,128]{2,1,0:T(8,128)(4,1)} %reshape.181) | copy-start | bytes 110596
  332.1 16.0 %collective-permute-start.1 = (bf16[128,32,128]{2,0,1:T(8,128)(2,1)S(1)}, bf16[128,32,128]{2,0,1:T(8,128)(2,1)S(1)}, u32[]{:S(2)}, u32[]{:S(2)}) collective-permute-start(bf16[128,32,128]{2,0,1:T(8,128)(2,1)S(1)} %fusion.31), channel_id=1, source_target_pairs={{0,120},{8,0},{16,8},{24,16},{32,24},{40,32},{48,40},{56,48},{64,5... | collective-permute-start | bytes 3145736 | tf_op jit(solution)/shard_map/ppermute | solution.py:9
  348.6 12.4 %copy-start.10 = (bf16[8,36,32,128]{3,2,1,0:T(8,128)(2,1)S(1)}, bf16[8,36,32,128]{3,2,1,0:T(8,128)(2,1)}, u32[]{:S(2)}) copy-start(bf16[8,36,32,128]{3,2,1,0:T(8,128)(2,1)} %copy-done.9) | copy-start | bytes 7077892
  349.9 28.5 %all-to-all-start.8 = ((bf16[8,576,128]{2,1,0:T(8,128)(2,1)}), bf16[8,576,128]{2,1,0:T(8,128)(2,1)}, u32[]{:S(2)}, u32[]{:S(2)}) async-start(bf16[8,576,128]{2,1,0:T(8,128)(2,1)} %bitcast.116), calls=%async_computation.8 | async-start | bytes 2359296 | tf_op jit(solution)/shard_map/all_to_all | solution.py:63
  361.0 7.6 %copy-start.20 = (pred[8,36,128]{2,1,0:T(8,128)(4,1)S(1)}, pred[8,36,128]{2,1,0:T(8,128)(4,1)}, u32[]{:S(2)}) copy-start(pred[8,36,128]{2,1,0:T(8,128)(4,1)} %reshape.181) | copy-start | bytes 110596
  378.4 20.8 %all-to-all-start.10 = ((bf16[8,576,128]{2,1,0:T(8,128)(2,1)}), bf16[8,576,128]{2,1,0:T(8,128)(2,1)S(1)}, u32[]{:S(2)}, u32[]{:S(2)}) async-start(bf16[8,576,128]{2,1,0:T(8,128)(2,1)} %bitcast.139), calls=%async_computation.10 | async-start | bytes 2359296 | tf_op jit(solution)/shard_map/all_to_all | solution.py:63
  382.0 6.9 %copy-start.11 = (f32[8,36,768]{2,1,0:T(8,128)S(1)}, f32[8,36,768]{2,1,0:T(8,128)}, u32[]{:S(2)}) copy-start(f32[8,36,768]{2,1,0:T(8,128)} %fusion.75) | copy-start | bytes 2654212
  382.0 6.9 %copy-start.22 = (f32[8,36,768]{2,1,0:T(8,128)S(1)}, f32[8,36,768]{2,1,0:T(8,128)}, u32[]{:S(2)}) copy-start(f32[8,36,768]{2,1,0:T(8,128)} %fusion.72) | copy-start | bytes 2654212
  382.0 11.4 %slice-start.10 = ((s8[6291456]{0:T(1024)(128)(4,1)}), s8[4194304]{0:T(1024)(128)(4,1)S(1)}, s32[]{:S(2)}) async-start(s8[6291456]{0:T(1024)(128)(4,1)} %bitcast.380), calls=%async_computation.22 | async-start | bytes 8388608
  400.2 21.0 %all-to-all-start.9 = ((bf16[8,576,128]{2,1,0:T(8,128)(2,1)}), bf16[8,576,128]{2,1,0:T(8,128)(2,1)S(1)}, u32[]{:S(2)}, u32[]{:S(2)}) async-start(bf16[8,576,128]{2,1,0:T(8,128)(2,1)} %bitcast.129), calls=%async_computation.9 | async-start | bytes 2359296 | tf_op jit(solution)/shard_map/all_to_all | solution.py:63
  404.0 6.9 %copy-start.23 = (f32[8,36,768]{2,1,0:T(8,128)S(1)}, f32[8,36,768]{2,1,0:T(8,128)}, u32[]{:S(2)}) copy-start(f32[8,36,768]{2,1,0:T(8,128)} %fusion.72) | copy-start | bytes 2654212
  404.1 11.5 %slice-start.12 = ((s8[6291456]{0:T(1024)(128)(4,1)}), s8[4194304]{0:T(1024)(128)(4,1)S(1)}, s32[]{:S(2)}) async-start(s8[6291456]{0:T(1024)(128)(4,1)} %bitcast.383), calls=%async_computation.24 | async-start | bytes 8388608
  421.2 20.8 %all-to-all-start.11 = ((bf16[8,576,128]{2,1,0:T(8,128)(2,1)}), bf16[8,576,128]{2,1,0:T(8,128)(2,1)S(1)}, u32[]{:S(2)}, u32[]{:S(2)}) async-start(bf16[8,576,128]{2,1,0:T(8,128)(2,1)} %bitcast.407), calls=%async_computation.11 | async-start | bytes 2359296 | tf_op jit(solution)/shard_map/all_to_all | solution.py:63
  446.3 15.8 %collective-permute-start.2 = (bf16[128,32,128]{2,0,1:T(8,128)(2,1)S(1)}, bf16[128,32,128]{2,0,1:T(8,128)(2,1)S(1)}, u32[]{:S(2)}, u32[]{:S(2)}) collective-permute-start(bf16[128,32,128]{2,0,1:T(8,128)(2,1)S(1)} %fusion.30), channel_id=1, source_target_pairs={{0,120},{8,0},{16,8},{24,16},{32,24},{40,32},{48,40},{56,48},{64,5... | collective-permute-start | bytes 3145736 | tf_op jit(solution)/shard_map/ppermute | solution.py:9
  (28 other events, 96.1 us)

commit v2 on v0

--- a/solution.py
+++ b/solution.py
@@ -63,9 +63,23 @@
         moved = lax.all_to_all(flat, "expert", split_axis=0, concat_axis=0, tiled=True)
         return moved.reshape(groups, count, pieces, lanes)
 
+    def send_around(buffer):
+        parts = [buffer[0]] + [
+            lax.ppermute(buffer[k], "expert", [(i, (i + k) % groups) for i in range(groups)])
+            for k in range(1, groups)
+        ]
+        return jnp.stack(parts)
+
+    position = lax.axis_index("expert")
+    rotation = (position + jnp.arange(groups, dtype=jnp.int32)) % groups
+    restore = (position - jnp.arange(groups, dtype=jnp.int32)) % groups
+
     plans = [route_plan(step) for step in range(rounds)]
     input_buffers = [
-        collect(plans[step][0], saved_inputs[step, 0].reshape(rows_dev, pieces, lanes))
+        collect(
+            plans[step][0] if step == 0 else jnp.take(plans[step][0], rotation, axis=0),
+            saved_inputs[step, 0].reshape(rows_dev, pieces, lanes),
+        )
         for step in range(rounds)
     ]
     first_part = exchange(input_buffers[0])
@@ -76,11 +90,14 @@
     present_block = first_block.reshape(rows_dev, pieces, lanes)
     for step in range(rounds):
         dispatch, weights_hi, weights_lo = plans[step]
-        if step > 0:
-            next_part, present_block = lax.optimization_barrier((next_part, present_block))
         grad_parts = [exchange(collect(dispatch[:, lo:hi], present_block)) for lo, hi in bounds]
         if step > 0:
             pre_gate, pre_up = forward_part(next_part, gate_proj, up_proj)
+            pre_gate = jnp.take(pre_gate, restore, axis=0)
+            pre_up = jnp.take(pre_up, restore, axis=0)
+        if step + 1 < rounds:
+            grad_parts[0], next_buffer = lax.optimization_barrier((grad_parts[0], input_buffers[step + 1]))
+            next_part = send_around(next_buffer)
         results = [
             backward_part(grad_parts[i], pre_gate[:, lo:hi], pre_up[:, lo:hi], gate_proj, up_proj, down_proj)
             for i, (lo, hi) in enumerate(bounds)
@@ -88,9 +105,6 @@
         summed = present_block.astype(jnp.float32)
         for i, (lo, hi) in enumerate(bounds):
             arrived = exchange(results[i])
-            if i + 1 == len(bounds) and step + 1 < rounds:
-                arrived, next_buffer = lax.optimization_barrier((arrived, input_buffers[step + 1]))
-                next_part = exchange(next_buffer)
             summed = summed + jnp.einsum(
                 "tec,ecjl->tjl", weights_hi[:, :, lo:hi], arrived, preferred_element_type=jnp.float32
             )

time: 433 us -> 462 us (1.067)
  the two profiles are of different devices: /device:TPU:7 before, /device:TPU:1 now
where the time goes in v2:
time: 462 us; the launch traced here: 455 us
  waiting for transfers between devices  156 us (34%)
  matrix products  137 us (30%)
  starting transfers between devices  81.6 us (18%)
  local copies, waits for them, and re-layouts  72.9 us (16%)
  other arithmetic  5.66 us (1%)
    all_to_all x13, waiting for transfers between devices, exchange(): lax.all_to_all(flat, 'expert', split_axis=0, concat_axis=0, tiled=True)  80.4 us
    all_to_all x13, starting transfers between devices, exchange(): lax.all_to_all(flat, 'expert', split_axis=0, concat_axis=0, tiled=True)  59.5 us
    dot_general x6, matrix products, backward_part(): jnp.einsum('scjl,hjl->sch', grad_part, down_proj, preferred_element_type=...  42.2 us
    ppermute x14, waiting for transfers between devices, send_around(): lax.ppermute(buffer[k], 'expert', [(i, (i + k) % groups) for i in range(g...  38.7 us
    ppermute x3, waiting for transfers between devices, shifted(): lax.ppermute(x, axis, [(i, (i + by) % devices) for i in range(devices)])  36.8 us
    unnamed x133, local copies, waits for them, and re-layouts  32.3 us
    dot_general x6, matrix products, backward_part(): jnp.einsum('sch,jlh->scjl', grad_gate, gate_proj, preferred_element_type=...  27.7 us
    dot_general x3, matrix products, forward_part(): jnp.einsum('scjl,jlh->sch', input_part, up_proj, preferred_element_type=j...  16.6 us
  transfers between devices with their start and end apart: 30, of which 20 were waited for; matrix products, arithmetic and copies ran while one was open for 36% of the time, Pallas kernels for 0%

profile of v2, /device:TPU:1, one launch (start us, length us, event | category | flops | bytes accessed | tf_op | source)
XLA Modules:
  0.0 454.5 jit_solution(10712842439693729149)
XLA Ops:
  7.6 6.4 %all-to-all-start = ((bf16[8,1152,128]{2,1,0:T(8,128)(2,1)}), bf16[8,1152,128]{2,1,0:T(8,128)(2,1)}, u32[]{:S(2)}, u32[]{:S(2)}) async-start(bf16[8,1152,128]{2,1,0:T(8,128)(2,1)} %bitcast.5), calls=%async_computation | async-start | bytes 4718592 | tf_op jit(solution)/shard_map/all_to_all | solution.py:63
  14.6 7.4 %copy.187 = bf16[96,8,32,128]{3,2,1,0:T(8,128)(2,1)} copy(bf16[96,8,32,128]{3,1,2,0:T(8,128)(2,1)} %bitcast.468) | data formatting | bytes 12582912
  37.5 6.4 %all-to-all-done = bf16[8,1152,128]{2,1,0:T(8,128)(2,1)} async-done(((bf16[8,1152,128]{2,1,0:T(8,128)(2,1)}), bf16[8,1152,128]{2,1,0:T(8,128)(2,1)}, u32[]{:S(2)}, u32[]{:S(2)}) %all-to-all-start) | async-done | bytes 2359328 | tf_op jit(solution)/shard_map/all_to_all | solution.py:63
  46.4 6.3 %all-to-all-start.3 = ((bf16[8,576,128]{2,1,0:T(8,128)(2,1)}), bf16[8,576,128]{2,1,0:T(8,128)(2,1)}, u32[]{:S(2)}, u32[]{:S(2)}) async-start(bf16[8,576,128]{2,1,0:T(8,128)(2,1)} %bitcast.480), calls=%async_computation.3 | async-start | bytes 2359296 | tf_op jit(solution)/shard_map/all_to_all | solution.py:63
  54.0 7.5 %fusion.52 = f32[8,36,768]{2,1,0:T(8,128)} fusion(bf16[32,128,768,1]{2,1,0,3:T(8,128)(2,1)} %bitcast.430, bf16[8,36,32,128]{3,2,1,0:T(8,128)(2,1)} %bitcast.6), kind=kOutput, calls=%fused_computation.85 | convolution fusion | flops 1811939328 | bytes 9535488 | tf_op jit(solution)/shard_map/scjl,jlh->sch/dot_general | solution.py:14
  73.6 6.8 %fusion.63 = f32[8,18,768]{2,1,0:T(8,128)S(1)} fusion(bf16[768,32,128]{2,1,0:T(8,128)(2,1)} %bitcast.469, bf16[8,18,32,128]{3,2,1,0:T(8,128)(2,1)} %bitcast.50), kind=kOutput, calls=%fused_computation.92 | convolution fusion | flops 905969664 | bytes 7913472 | tf_op jit(solution)/shard_map/scjl,hjl->sch/dot_general | solution.py:19
  80.5 4.6 %fusion.117 = f32[8,18,32,128]{3,1,2,0:T(8,128)S(1)} fusion(bf16[32,128,768,1]{2,1,0,3:T(8,128)(2,1)} %bitcast.493, f32[8,18,768]{2,1,0:T(8,128)S(1)} %fusion.63, f32[8,36,768]{2,1,0:T(8,128)S(1)} %copy-done.38, f32[8,36,768]{2,1,0:T(8,128)S(1)} %fusion.55), kind=kOutput, calls=%fused_computation.178 | convolution fusion | flops 907075584 | bytes 10420224 | tf_op jit(solution)/shard_map/sch,jlh->scjl/dot_general | solution.py:24
  95.6 6.8 %fusion.58 = f32[8,18,768]{2,1,0:T(8,128)S(1)} fusion(bf16[768,32,128]{2,1,0:T(8,128)(2,1)} %bitcast.470, bf16[8,18,32,128]{3,2,1,0:T(8,128)(2,1)} %bitcast.487), kind=kOutput, calls=%fused_computation.91 | convolution fusion | flops 905969664 | bytes 7913472 | tf_op jit(solution)/shard_map/scjl,hjl->sch/dot_general | solution.py:19
  102.4 4.5 fusion.120
  114.3 4.6 %all-to-all-start.2 = ((bf16[8,576,128]{2,1,0:T(8,128)(2,1)}), bf16[8,576,128]{2,1,0:T(8,128)(2,1)S(1)}, u32[]{:S(2)}, u32[]{:S(2)}) async-start(bf16[8,576,128]{2,1,0:T(8,128)(2,1)} %bitcast.475), calls=%async_computation.2 | async-start | bytes 2359296 | tf_op jit(solution)/shard_map/all_to_all | solution.py:63
  129.8 16.4 %collective-permute-done.2 = bf16[36,32,128]{2,0,1:T(8,128)(2,1)} collective-permute-done((bf16[36,32,128]{2,0,1:T(8,128)(2,1)}, bf16[36,32,128]{2,0,1:T(8,128)(2,1)}, u32[]{:S(2)}, u32[]{:S(2)}) %collective-permute-start.2) | collective-permute-done | bytes 294944 | tf_op jit(solution)/shard_map/ppermute | solution.py:68
  166.7 7.0 %collective-permute-done = bf16[128,32,128]{2,0,1:T(8,128)(2,1)S(1)} collective-permute-done((bf16[128,32,128]{2,0,1:T(8,128)(2,1)S(1)}, bf16[128,32,128]{2,0,1:T(8,128)(2,1)S(1)}, u32[]{:S(2)}, u32[]{:S(2)}) %collective-permute-start) | collective-permute-done | bytes 1048608 | tf_op jit(solution)/shard_map/ppermute | solution.py:9
  175.5 8.5 %all-to-all-start.7 = ((bf16[8,576,128]{2,1,0:T(8,128)(2,1)}), bf16[8,576,128]{2,1,0:T(8,128)(2,1)S(1)}, u32[]{:S(2)}, u32[]{:S(2)}) async-start(bf16[8,576,128]{2,1,0:T(8,128)(2,1)} %bitcast.114), calls=%async_computation.7 | async-start | bytes 2359296 | tf_op jit(solution)/shard_map/all_to_all | solution.py:63
  183.9 5.8 %convolution_bitcast_fusion.2 = f32[8,36,768]{2,1,0:T(8,128)S(1)} fusion(bf16[8,36,32,128]{3,1,2,0:T(8,128)(2,1)} %bitcast_dynamic-update-slice_fusion.7, bf16[32,128,768,1]{2,1,0,3:T(8,128)(2,1)} %bitcast.495), kind=kOutput, calls=%fused_computation.89 | convolution fusion | flops 1811939328 | bytes 9535488 | tf_op jit(solution)/shard_map/scjl,jlh->sch/dot_general | solution.py:13
  191.6 9.6 %all-to-all-done.7 = bf16[8,576,128]{2,1,0:T(8,128)(2,1)S(1)} async-done(((bf16[8,576,128]{2,1,0:T(8,128)(2,1)}), bf16[8,576,128]{2,1,0:T(8,128)(2,1)S(1)}, u32[]{:S(2)}, u32[]{:S(2)}) %all-to-all-start.7) | async-done | bytes 1179680 | tf_op jit(solution)/shard_map/all_to_all | solution.py:63
  205.4 5.8 %convolution_bitcast_fusion.3 = f32[8,36,768]{2,1,0:T(8,128)S(1)} fusion(bf16[8,36,32,128]{3,1,2,0:T(8,128)(2,1)} %bitcast_dynamic-update-slice_fusion.7, bf16[32,128,768,1]{2,1,0,3:T(8,128)(2,1)} %bitcast.431), kind=kOutput, calls=%fused_computation.90 | convolution fusion | flops 1811939328 | bytes 9535488 | tf_op jit(solution)/shard_map/scjl,jlh->sch/dot_general | solution.py:14
  214.4 6.8 %fusion.73 = f32[8,18,768]{2,1,0:T(8,128)S(1)} fusion(bf16[768,32,128]{2,1,0:T(8,128)(2,1)} %bitcast.471, bf16[8,18,32,128]{3,2,1,0:T(8,128)(2,1)} %bitcast.485), kind=kOutput, calls=%fused_computation.94 | convolution fusion | flops 905969664 | bytes 7913472 | tf_op jit(solution)/shard_map/scjl,hjl->sch/dot_general | solution.py:19
  229.2 8.0 %fusion.68 = f32[8,18,768]{2,1,0:T(8,128)} fusion(bf16[768,32,128]{2,1,0:T(8,128)(2,1)} %bitcast.472, bf16[8,18,32,128]{3,2,1,0:T(8,128)(2,1)} %bitcast.72), kind=kOutput, calls=%fused_computation.93 | convolution fusion | flops 905969664 | bytes 7913472 | tf_op jit(solution)/shard_map/scjl,hjl->sch/dot_general | solution.py:19
  242.7 4.5 collective-permute-done.11
  247.3 8.7 %collective-permute-done.12 = bf16[36,32,128]{2,0,1:T(8,128)(2,1)S(1)} collective-permute-done((bf16[36,32,128]{2,0,1:T(8,128)(2,1)S(1)}, bf16[36,32,128]{2,0,1:T(8,128)(2,1)S(1)}, u32[]{:S(2)}, u32[]{:S(2)}) %collective-permute-start.12) | collective-permute-done | bytes 294944 | tf_op jit(solution)/shard_map/ppermute | solution.py:68
  276.4 4.6 %fusion.111 = f32[8,18,32,128]{3,1,2,0:T(8,128)S(1)} fusion(bf16[32,128,768,1]{2,1,0,3:T(8,128)(2,1)} %bitcast.496, f32[8,18,768]{2,1,0:T(8,128)S(1)} %fusion.73, f32[8,36,768]{2,1,0:T(8,128)S(1)} %get-tuple-element.53, f32[8,36,768]{2,1,0:T(8,128)S(1)} %get-tuple-element.51), kind=kOutput, calls=%fused_computation.172 | convolution fusion | flops 907075584 | bytes 10420224 | tf_op jit(solution)/shard_map/sch,jlh->scjl/dot_general | solution.py:24
  288.4 4.9 %fusion.114 = f32[8,18,32,128]{3,1,2,0:T(8,128)S(1)} fusion(bf16[32,128,768,1]{2,1,0,3:T(8,128)(2,1)} %bitcast.497, f32[8,18,768]{2,1,0:T(8,128)} %fusion.68, f32[8,36,768]{2,1,0:T(8,128)} %copy-done.21, f32[8,36,768]{2,1,0:T(8,128)} %copy-done.8), kind=kOutput, calls=%fused_computation.175 | convolution fusion | flops 907075584 | bytes 10420224 | tf_op jit(solution)/shard_map/sch,jlh->scjl/dot_general | solution.py:24
  297.0 8.6 %all-to-all-done.8 = bf16[8,576,128]{2,1,0:T(8,128)(2,1)S(1)} async-done(((bf16[8,576,128]{2,1,0:T(8,128)(2,1)}), bf16[8,576,128]{2,1,0:T(8,128)(2,1)S(1)}, u32[]{:S(2)}, u32[]{:S(2)}) %all-to-all-start.8) | async-done | bytes 1179680 | tf_op jit(solution)/shard_map/all_to_all | solution.py:63
  311.3 15.1 %all-to-all-done.6 = bf16[8,576,128]{2,1,0:T(8,128)(2,1)S(1)} async-done(((bf16[8,576,128]{2,1,0:T(8,128)(2,1)}), bf16[8,576,128]{2,1,0:T(8,128)(2,1)S(1)}, u32[]{:S(2)}, u32[]{:S(2)}) %all-to-all-start.6) | async-done | bytes 1179680 | tf_op jit(solution)/shard_map/all_to_all | solution.py:63
  330.7 14.9 %collective-permute-done.8 = bf16[128,32,128]{2,0,1:T(8,128)(2,1)S(1)} collective-permute-done((bf16[128,32,128]{2,0,1:T(8,128)(2,1)S(1)}, bf16[128,32,128]{2,0,1:T(8,128)(2,1)S(1)}, u32[]{:S(2)}, u32[]{:S(2)}) %collective-permute-start.8) | collective-permute-done | bytes 1048608 | tf_op jit(solution)/shard_map/ppermute | solution.py:9
  352.9 15.5 %all-to-all-done.11 = bf16[8,576,128]{2,1,0:T(8,128)(2,1)S(1)} async-done(((bf16[8,576,128]{2,1,0:T(8,128)(2,1)}), bf16[8,576,128]{2,1,0:T(8,128)(2,1)S(1)}, u32[]{:S(2)}, u32[]{:S(2)}) %all-to-all-start.11) | async-done | bytes 1179680 | tf_op jit(solution)/shard_map/all_to_all | solution.py:63
  372.2 6.8 %fusion.83 = f32[8,18,768]{2,1,0:T(8,128)S(1)} fusion(bf16[768,32,128]{2,1,0:T(8,128)(2,1)} %bitcast.473, bf16[8,18,32,128]{3,2,1,0:T(8,128)(2,1)} %bitcast.488), kind=kOutput, calls=%fused_computation.96 | convolution fusion | flops 905969664 | bytes 7913472 | tf_op jit(solution)/shard_map/scjl,hjl->sch/dot_general | solution.py:19
  379.1 4.6 %fusion.105 = f32[8,18,32,128]{3,1,2,0:T(8,128)S(1)} fusion(bf16[32,128,768,1]{2,1,0,3:T(8,128)(2,1)} %bitcast.498, f32[8,18,768]{2,1,0:T(8,128)S(1)} %fusion.83, f32[8,36,768]{2,1,0:T(8,128)S(1)} %copy-done.19, f32[8,36,768]{2,1,0:T(8,128)S(1)} %copy-done.7), kind=kOutput, calls=%fused_computation.166 | convolution fusion | flops 907075584 | bytes 10420224 | tf_op jit(solution)/shard_map/sch,jlh->scjl/dot_general | solution.py:24
  394.0 6.8 %fusion.78 = f32[8,18,768]{2,1,0:T(8,128)S(1)} fusion(bf16[768,32,128]{2,1,0:T(8,128)(2,1)} %bitcast.474, bf16[8,18,32,128]{3,2,1,0:T(8,128)(2,1)} %bitcast.486), kind=kOutput, calls=%fused_computation.95 | convolution fusion | flops 905969664 | bytes 7913472 | tf_op jit(solution)/shard_map/scjl,hjl->sch/dot_general | solution.py:19
  400.9 4.5 fusion.108
  419.3 13.0 %all-to-all-done.10 = bf16[8,576,128]{2,1,0:T(8,128)(2,1)S(1)} async-done(((bf16[8,576,128]{2,1,0:T(8,128)(2,1)}), bf16[8,576,128]{2,1,0:T(8,128)(2,1)S(1)}, u32[]{:S(2)}, u32[]{:S(2)}) %all-to-all-start.10) | async-done | bytes 1179680 | tf_op jit(solution)/shard_map/all_to_all | solution.py:63
  437.1 14.9 %collective-permute-done.16 = bf16[128,32,128]{2,0,1:T(8,128)(2,1)S(1)} collective-permute-done((bf16[128,32,128]{2,0,1:T(8,128)(2,1)S(1)}, bf16[128,32,128]{2,0,1:T(8,128)(2,1)S(1)}, u32[]{:S(2)}, u32[]{:S(2)}) %collective-permute-start.16) | collective-permute-done | bytes 1048608 | tf_op jit(solution)/shard_map/ppermute | solution.py:9
  (267 shorter events, 196.3 us)
Async XLA Ops:
  7.6 36.3 %all-to-all-start = ((bf16[8,1152,128]{2,1,0:T(8,128)(2,1)}), bf16[8,1152,128]{2,1,0:T(8,128)(2,1)}, u32[]{:S(2)}, u32[]{:S(2)}) async-start(bf16[8,1152,128]{2,1,0:T(8,128)(2,1)} %bitcast.5), calls=%async_computation | async-start | bytes 4718592 | tf_op jit(solution)/shard_map/all_to_all | solution.py:63
  46.4 23.6 %all-to-all-start.3 = ((bf16[8,576,128]{2,1,0:T(8,128)(2,1)}), bf16[8,576,128]{2,1,0:T(8,128)(2,1)}, u32[]{:S(2)}, u32[]{:S(2)}) async-start(bf16[8,576,128]{2,1,0:T(8,128)(2,1)} %bitcast.480), calls=%async_computation.3 | async-start | bytes 2359296 | tf_op jit(solution)/shard_map/all_to_all | solution.py:63
  70.0 20.7 %all-to-all-start.1 = ((bf16[8,576,128]{2,1,0:T(8,128)(2,1)}), bf16[8,576,128]{2,1,0:T(8,128)(2,1)S(1)}, u32[]{:S(2)}, u32[]{:S(2)}) async-start(bf16[8,576,128]{2,1,0:T(8,128)(2,1)} %bitcast.14), calls=%async_computation.1 | async-start | bytes 2359296 | tf_op jit(solution)/shard_map/all_to_all | solution.py:63
  91.8 22.6 %all-to-all-start.4 = ((bf16[8,576,128]{2,1,0:T(8,128)(2,1)}), bf16[8,576,128]{2,1,0:T(8,128)(2,1)S(1)}, u32[]{:S(2)}, u32[]{:S(2)}) async-start(bf16[8,576,128]{2,1,0:T(8,128)(2,1)} %bitcast.59), calls=%async_computation.4 | async-start | bytes 2359296 | tf_op jit(solution)/shard_map/all_to_all | solution.py:63
  112.9 14.0 %collective-permute-start.1 = (bf16[36,32,128]{2,0,1:T(8,128)(2,1)}, bf16[36,32,128]{2,0,1:T(8,128)(2,1)}, u32[]{:S(2)}, u32[]{:S(2)}) collective-permute-start(bf16[36,32,128]{2,0,1:T(8,128)(2,1)} %get-tuple-element.42), channel_id=1, source_target_pairs={{0,1},{1,2},{2,3},{3,4},{4,5},{5,6},{6,7},{7,0},{8,9},{9,10},{10,1... | collective-permute-start | bytes 884744 | tf_op jit(solution)/shard_map/ppermute | solution.py:68
  114.3 36.3 %all-to-all-start.2 = ((bf16[8,576,128]{2,1,0:T(8,128)(2,1)}), bf16[8,576,128]{2,1,0:T(8,128)(2,1)S(1)}, u32[]{:S(2)}, u32[]{:S(2)}) async-start(bf16[8,576,128]{2,1,0:T(8,128)(2,1)} %bitcast.475), calls=%async_computation.2 | async-start | bytes 2359296 | tf_op jit(solution)/shard_map/all_to_all | solution.py:63
  119.0 27.2 %collective-permute-start.2 = (bf16[36,32,128]{2,0,1:T(8,128)(2,1)}, bf16[36,32,128]{2,0,1:T(8,128)(2,1)}, u32[]{:S(2)}, u32[]{:S(2)}) collective-permute-start(bf16[36,32,128]{2,0,1:T(8,128)(2,1)} %get-tuple-element.41), channel_id=1, source_target_pairs={{0,2},{1,3},{2,4},{3,5},{4,6},{5,7},{6,0},{7,1},{8,10},{9,11},{10,... | collective-permute-start | bytes 884744 | tf_op jit(solution)/shard_map/ppermute | solution.py:68
  123.3 30.7 %collective-permute-start.3 = (bf16[36,32,128]{2,0,1:T(8,128)(2,1)}, bf16[36,32,128]{2,0,1:T(8,128)(2,1)}, u32[]{:S(2)}, u32[]{:S(2)}) collective-permute-start(bf16[36,32,128]{2,0,1:T(8,128)(2,1)} %get-tuple-element.40), channel_id=1, source_target_pairs={{0,3},{1,4},{2,5},{3,6},{4,7},{5,0},{6,1},{7,2},{8,11},{9,12},{10,... | collective-permute-start | bytes 884744 | tf_op jit(solution)/shard_map/ppermute | solution.py:68
  125.1 34.6 %collective-permute-start.4 = (bf16[36,32,128]{2,0,1:T(8,128)(2,1)}, bf16[36,32,128]{2,0,1:T(8,128)(2,1)}, u32[]{:S(2)}, u32[]{:S(2)}) collective-permute-start(bf16[36,32,128]{2,0,1:T(8,128)(2,1)} %get-tuple-element.39), channel_id=1, source_target_pairs={{0,4},{1,5},{2,6},{3,7},{4,0},{5,1},{6,2},{7,3},{8,12},{9,13},{10,... | collective-permute-start | bytes 884744 | tf_op jit(solution)/shard_map/ppermute | solution.py:68
  125.4 36.0 %collective-permute-start.5 = (bf16[36,32,128]{2,0,1:T(8,128)(2,1)}, bf16[36,32,128]{2,0,1:T(8,128)(2,1)}, u32[]{:S(2)}, u32[]{:S(2)}) collective-permute-start(bf16[36,32,128]{2,0,1:T(8,128)(2,1)} %get-tuple-element.38), channel_id=1, source_target_pairs={{0,5},{1,6},{2,7},{3,0},{4,1},{5,2},{6,3},{7,4},{8,13},{9,14},{10,... | collective-permute-start | bytes 884744 | tf_op jit(solution)/shard_map/ppermute | solution.py:68
  126.9 36.3 %collective-permute-start.6 = (bf16[36,32,128]{2,0,1:T(8,128)(2,1)}, bf16[36,32,128]{2,0,1:T(8,128)(2,1)}, u32[]{:S(2)}, u32[]{:S(2)}) collective-permute-start(bf16[36,32,128]{2,0,1:T(8,128)(2,1)} %get-tuple-element.37), channel_id=1, source_target_pairs={{0,6},{1,7},{2,0},{3,1},{4,2},{5,3},{6,4},{7,5},{8,14},{9,15},{10,... | collective-permute-start | bytes 884744 | tf_op jit(solution)/shard_map/ppermute | solution.py:68
  146.2 18.7 %collective-permute-start.7 = (bf16[36,32,128]{2,0,1:T(8,128)(2,1)}, bf16[36,32,128]{2,0,1:T(8,128)(2,1)}, u32[]{:S(2)}, u32[]{:S(2)}) collective-permute-start(bf16[36,32,128]{2,0,1:T(8,128)(2,1)} %get-tuple-element.36), channel_id=1, source_target_pairs={{0,7},{1,0},{2,1},{3,2},{4,3},{5,4},{6,5},{7,6},{8,15},{9,8},{10,9... | collective-permute-start | bytes 884744 | tf_op jit(solution)/shard_map/ppermute | solution.py:68
  154.0 19.6 %collective-permute-start = (bf16[128,32,128]{2,0,1:T(8,128)(2,1)S(1)}, bf16[128,32,128]{2,0,1:T(8,128)(2,1)S(1)}, u32[]{:S(2)}, u32[]{:S(2)}) collective-permute-start(bf16[128,32,128]{2,0,1:T(8,128)(2,1)S(1)} %fusion.24), channel_id=1, source_target_pairs={{0,120},{8,0},{16,8},{24,16},{32,24},{40,32},{48,40},{56,48},{64,5... | collective-permute-start | bytes 3145736 | tf_op jit(solution)/shard_map/ppermute | solution.py:9
  175.5 25.7 %all-to-all-start.7 = ((bf16[8,576,128]{2,1,0:T(8,128)(2,1)}), bf16[8,576,128]{2,1,0:T(8,128)(2,1)S(1)}, u32[]{:S(2)}, u32[]{:S(2)}) async-start(bf16[8,576,128]{2,1,0:T(8,128)(2,1)} %bitcast.114), calls=%async_computation.7 | async-start | bytes 2359296 | tf_op jit(solution)/shard_map/all_to_all | solution.py:63
  201.1 21.5 %all-to-all-start.5 = ((bf16[8,576,128]{2,1,0:T(8,128)(2,1)}), bf16[8,576,128]{2,1,0:T(8,128)(2,1)}, u32[]{:S(2)}, u32[]{:S(2)}) async-start(bf16[8,576,128]{2,1,0:T(8,128)(2,1)} %bitcast.71), calls=%async_computation.5 | async-start | bytes 2359296 | tf_op jit(solution)/shard_map/all_to_all | solution.py:63
  223.1 14.1 %collective-permute-start.9 = (bf16[36,32,128]{2,0,1:T(8,128)(2,1)S(1)}, bf16[36,32,128]{2,0,1:T(8,128)(2,1)S(1)}, u32[]{:S(2)}, u32[]{:S(2)}) collective-permute-start(bf16[36,32,128]{2,0,1:T(8,128)(2,1)S(1)} %get-tuple-element.34), channel_id=1, source_target_pairs={{0,1},{1,2},{2,3},{3,4},{4,5},{5,6},{6,7},{7,0},{8,9},{9,10},{10,1... | collective-permute-start | bytes 884744 | tf_op jit(solution)/shard_map/ppermute | solution.py:68
  223.2 19.5 %collective-permute-start.10 = (bf16[36,32,128]{2,0,1:T(8,128)(2,1)S(1)}, bf16[36,32,128]{2,0,1:T(8,128)(2,1)S(1)}, u32[]{:S(2)}, u32[]{:S(2)}) collective-permute-start(bf16[36,32,128]{2,0,1:T(8,128)(2,1)S(1)} %get-tuple-element.33), channel_id=1, source_target_pairs={{0,2},{1,3},{2,4},{3,5},{4,6},{5,7},{6,0},{7,1},{8,10},{9,11},{10,... | collective-permute-start | bytes 884744 | tf_op jit(solution)/shard_map/ppermute | solution.py:68
  225.5 21.7 %collective-permute-start.11 = (bf16[36,32,128]{2,0,1:T(8,128)(2,1)S(1)}, bf16[36,32,128]{2,0,1:T(8,128)(2,1)S(1)}, u32[]{:S(2)}, u32[]{:S(2)}) collective-permute-start(bf16[36,32,128]{2,0,1:T(8,128)(2,1)S(1)} %get-tuple-element.32), channel_id=1, source_target_pairs={{0,3},{1,4},{2,5},{3,6},{4,7},{5,0},{6,1},{7,2},{8,11},{9,12},{10,... | collective-permute-start | bytes 884744 | tf_op jit(solution)/shard_map/ppermute | solution.py:68
  227.6 28.4 %collective-permute-start.12 = (bf16[36,32,128]{2,0,1:T(8,128)(2,1)S(1)}, bf16[36,32,128]{2,0,1:T(8,128)(2,1)S(1)}, u32[]{:S(2)}, u32[]{:S(2)}) collective-permute-start(bf16[36,32,128]{2,0,1:T(8,128)(2,1)S(1)} %get-tuple-element.31), channel_id=1, source_target_pairs={{0,4},{1,5},{2,6},{3,7},{4,0},{5,1},{6,2},{7,3},{8,12},{9,13},{10,... | collective-permute-start | bytes 884744 | tf_op jit(solution)/shard_map/ppermute | solution.py:68
  227.8 33.3 %slice-start.16 = ((s8[6291456]{0:T(1024)(128)(4,1)}), s8[4194304]{0:T(1024)(128)(4,1)S(1)}, s32[]{:S(2)}) async-start(s8[6291456]{0:T(1024)(128)(4,1)} %bitcast.503), calls=%async_computation.29 | async-start | bytes 8388608
  227.8 33.3 %slice-start.17 = ((s8[6291456]{0:T(1024)(128)(4,1)}), s8[2097152]{0:T(1024)(128)(4,1)S(1)}, s32[]{:S(2)}) async-start(s8[6291456]{0:T(1024)(128)(4,1)} %bitcast.503), calls=%async_computation.30 | async-start | bytes 4194304
  227.9 28.6 %collective-permute-start.13 = (bf16[36,32,128]{2,0,1:T(8,128)(2,1)S(1)}, bf16[36,32,128]{2,0,1:T(8,128)(2,1)S(1)}, u32[]{:S(2)}, u32[]{:S(2)}) collective-permute-start(bf16[36,32,128]{2,0,1:T(8,128)(2,1)S(1)} %get-tuple-element.30), channel_id=1, source_target_pairs={{0,5},{1,6},{2,7},{3,0},{4,1},{5,2},{6,3},{7,4},{8,13},{9,14},{10,... | collective-permute-start | bytes 884744 | tf_op jit(solution)/shard_map/ppermute | solution.py:68
  237.2 19.3 %collective-permute-start.14 = (bf16[36,32,128]{2,0,1:T(8,128)(2,1)S(1)}, bf16[36,32,128]{2,0,1:T(8,128)(2,1)S(1)}, u32[]{:S(2)}, u32[]{:S(2)}) collective-permute-start(bf16[36,32,128]{2,0,1:T(8,128)(2,1)S(1)} %get-tuple-element.29), channel_id=1, source_target_pairs={{0,6},{1,7},{2,0},{3,1},{4,2},{5,3},{6,4},{7,5},{8,14},{9,15},{10,... | collective-permute-start | bytes 884744 | tf_op jit(solution)/shard_map/ppermute | solution.py:68
  242.7 18.4 %collective-permute-start.15 = (bf16[36,32,128]{2,0,1:T(8,128)(2,1)S(1)}, bf16[36,32,128]{2,0,1:T(8,128)(2,1)S(1)}, u32[]{:S(2)}, u32[]{:S(2)}) collective-permute-start(bf16[36,32,128]{2,0,1:T(8,128)(2,1)S(1)} %get-tuple-element.28), channel_id=1, source_target_pairs={{0,7},{1,0},{2,1},{3,2},{4,3},{5,4},{6,5},{7,6},{8,15},{9,8},{10,9... | collective-permute-start | bytes 884744 | tf_op jit(solution)/shard_map/ppermute | solution.py:68
  284.6 21.0 %all-to-all-start.8 = ((bf16[8,576,128]{2,1,0:T(8,128)(2,1)}), bf16[8,576,128]{2,1,0:T(8,128)(2,1)S(1)}, u32[]{:S(2)}, u32[]{:S(2)}) async-start(bf16[8,576,128]{2,1,0:T(8,128)(2,1)} %bitcast.479), calls=%async_computation.8 | async-start | bytes 2359296 | tf_op jit(solution)/shard_map/all_to_all | solution.py:63
  305.6 20.7 %all-to-all-start.6 = ((bf16[8,576,128]{2,1,0:T(8,128)(2,1)}), bf16[8,576,128]{2,1,0:T(8,128)(2,1)S(1)}, u32[]{:S(2)}, u32[]{:S(2)}) async-start(bf16[8,576,128]{2,1,0:T(8,128)(2,1)} %bitcast.476), calls=%async_computation.6 | async-start | bytes 2359296 | tf_op jit(solution)/shard_map/all_to_all | solution.py:63
  329.8 15.8 %collective-permute-start.8 = (bf16[128,32,128]{2,0,1:T(8,128)(2,1)S(1)}, bf16[128,32,128]{2,0,1:T(8,128)(2,1)S(1)}, u32[]{:S(2)}, u32[]{:S(2)}) collective-permute-start(bf16[128,32,128]{2,0,1:T(8,128)(2,1)S(1)} %fusion.23), channel_id=1, source_target_pairs={{0,120},{8,0},{16,8},{24,16},{32,24},{40,32},{48,40},{56,48},{64,5... | collective-permute-start | bytes 3145736 | tf_op jit(solution)/shard_map/ppermute | solution.py:9
  347.5 20.8 %all-to-all-start.11 = ((bf16[8,576,128]{2,1,0:T(8,128)(2,1)}), bf16[8,576,128]{2,1,0:T(8,128)(2,1)S(1)}, u32[]{:S(2)}, u32[]{:S(2)}) async-start(bf16[8,576,128]{2,1,0:T(8,128)(2,1)} %bitcast.172), calls=%async_computation.11 | async-start | bytes 2359296 | tf_op jit(solution)/shard_map/all_to_all | solution.py:63
  368.4 21.0 %all-to-all-start.9 = ((bf16[8,576,128]{2,1,0:T(8,128)(2,1)}), bf16[8,576,128]{2,1,0:T(8,128)(2,1)S(1)}, u32[]{:S(2)}, u32[]{:S(2)}) async-start(bf16[8,576,128]{2,1,0:T(8,128)(2,1)} %bitcast.135), calls=%async_computation.9 | async-start | bytes 2359296 | tf_op jit(solution)/shard_map/all_to_all | solution.py:63
  390.4 20.8 %all-to-all-start.12 = ((bf16[8,576,128]{2,1,0:T(8,128)(2,1)}), bf16[8,576,128]{2,1,0:T(8,128)(2,1)S(1)}, u32[]{:S(2)}, u32[]{:S(2)}) async-start(bf16[8,576,128]{2,1,0:T(8,128)(2,1)} %bitcast.477), calls=%async_computation.12 | async-start | bytes 2359296 | tf_op jit(solution)/shard_map/all_to_all | solution.py:63
  411.2 21.1 %all-to-all-start.10 = ((bf16[8,576,128]{2,1,0:T(8,128)(2,1)}), bf16[8,576,128]{2,1,0:T(8,128)(2,1)S(1)}, u32[]{:S(2)}, u32[]{:S(2)}) async-start(bf16[8,576,128]{2,1,0:T(8,128)(2,1)} %bitcast.478), calls=%async_computation.10 | async-start | bytes 2359296 | tf_op jit(solution)/shard_map/all_to_all | solution.py:63
  436.3 15.8 %collective-permute-start.16 = (bf16[128,32,128]{2,0,1:T(8,128)(2,1)S(1)}, bf16[128,32,128]{2,0,1:T(8,128)(2,1)S(1)}, u32[]{:S(2)}, u32[]{:S(2)}) collective-permute-start(bf16[128,32,128]{2,0,1:T(8,128)(2,1)S(1)} %fusion.22), channel_id=1, source_target_pairs={{0,120},{8,0},{16,8},{24,16},{32,24},{40,32},{48,40},{56,48},{64,5... | collective-permute-start | bytes 3145736 | tf_op jit(solution)/shard_map/ppermute | solution.py:9
  (56 other events, 440.7 us)
